TPU v7x, 256 devices: a whole 4x4x8 slice. The times are simulated.
256 devices in a mesh: dp: 8 (over z), expert: 32 (over y, x, core).
Axes of the slice: x: 4, y: 4, z: 8, core: 2. Of those that a mesh axis runs over, the one named last changes fastest.
Arguments:
- tokens: bfloat16 [32, 64, 4096], P('expert'), may hold values from -6 to 6
- norm_gain: float32 [4096], replicated, may hold values from 0.25 to 1.75
- expert_ids: int32 [32, 64, 8], P('expert'), may hold values from 0 to 63, all different within a row; in each aligned block of 64 rows (0 to 63, 64 to 127, ..., all dimensions but the last counted through in order) at most 16 rows name the same one
- route_weights: float32 [32, 64, 8], P('expert'), may hold values from 0.02 to 0.4
- gate_proj: bfloat16 [64, 1536, 4096], P('expert', 'dp'), may hold values from -0.09375 to 0.09375
- up_proj: bfloat16 [64, 1536, 4096], P('expert', 'dp'), may hold values from -0.09375 to 0.09375
- down_proj: bfloat16 [64, 1536, 4096], P('expert', 'dp'), may hold values from -0.15625 to 0.15625
Outputs:
- mixed: bfloat16 [32, 64, 4096], P('expert', 'dp')
Inputs may be any that keep to these rules, and one draw needn't show every extreme that they name: `expert_ids`: each token names 8 different experts. Within one group no expert is named by more than 16 tokens, and in every draw some expert is named by exactly 16 tokens of some group.
All inputs are finite; a program needn't handle non-finite values.
Results may differ from a plain program's by a relative error of at most 0.019.
Values may be sent and summed in bfloat16 or wider, within the bound.
No kernel may reach another device: no remote copies, remote signals or barrier semaphores. Data moves between devices by JAX's collectives and lax.ppermute only.
A program may use at most 128 MiB of HBM per device.

v0:
```python
import jax
import jax.numpy as jnp
from jax import lax
from jax.sharding import PartitionSpec as P


def rank_slots(id_table, expert_total):
    flat_ids = id_table.reshape(-1)
    onehot = (flat_ids[:, None] == jnp.arange(expert_total, dtype=jnp.int32)[None, :]).astype(
        jnp.int32
    )
    before = jnp.cumsum(onehot, axis=0) - onehot
    return jnp.sum(before * onehot, axis=1).reshape(id_table.shape)


def body(tokens, norm_gain, expert_ids, route_weights, gate_proj, up_proj, down_proj):
    dp_count = lax.axis_size("dp")
    expert_count = lax.axis_size("expert")
    local_experts = gate_proj.shape[0]
    model_width = tokens.shape[2]
    group_ids = expert_ids[0]
    group_weights = route_weights[0]
    group_size = group_ids.shape[0]
    own_rows = group_size // dp_count
    top_k = group_ids.shape[1]
    experts = local_experts * expert_count
    capacity = dp_count * (group_size * top_k // (experts * dp_count) + 1)
    tok_float = tokens[0].astype(jnp.float32)
    inv_rms = lax.rsqrt(jnp.mean(tok_float * tok_float, axis=-1, keepdims=True) + 1e-06)
    group_rows = (tok_float * inv_rms * norm_gain).astype(jnp.bfloat16)
    slot_rank = rank_slots(group_ids, experts)
    slot_index = group_ids * capacity + slot_rank
    token_order = jnp.broadcast_to(
        jnp.arange(group_size, dtype=jnp.int32)[:, None], (group_size, top_k)
    )
    sources = (
        jnp.full((experts * capacity,), group_size, jnp.int32)
        .at[slot_index.reshape(-1)]
        .set(token_order.reshape(-1))
    )
    padded = jnp.concatenate([group_rows, jnp.zeros((1, model_width), jnp.bfloat16)], axis=0)
    outgoing = jnp.take(padded, sources, axis=0).reshape(
        expert_count, local_experts, capacity, model_width
    )
    incoming = lax.all_to_all(outgoing, "expert", split_axis=0, concat_axis=0, tiled=True)
    gate_act = jnp.einsum("sjmd,jfd->sjmf", incoming, gate_proj, preferred_element_type=jnp.float32)
    up_act = jnp.einsum("sjmd,jfd->sjmf", incoming, up_proj, preferred_element_type=jnp.float32)
    hidden = (jax.nn.silu(gate_act) * up_act).astype(jnp.bfloat16)
    partial_rows = jnp.einsum(
        "sjmf,jfd->sjmd", hidden, down_proj, preferred_element_type=jnp.float32
    ).astype(jnp.bfloat16)
    returned = lax.all_to_all(partial_rows, "expert", split_axis=0, concat_axis=0, tiled=True)
    lookup = jnp.concatenate(
        [
            returned.reshape(experts * capacity, model_width),
            jnp.zeros((1, model_width), jnp.bfloat16),
        ],
        axis=0,
    )
    picked = (
        jnp.take(lookup, slot_index.reshape(-1), axis=0)
        .reshape(own_rows * lax.axis_size("dp"), top_k, model_width)
        .astype(jnp.float32)
    )
    mixed = lax.psum_scatter(
        jnp.sum(picked * group_weights[:, :, None], axis=1).astype(jnp.bfloat16),
        "dp",
        scatter_dimension=0,
        tiled=True,
    )
    return mixed[None]


def solution(mesh):
    placed = (
        P("expert", None, None),
        P(),
        P("expert", None, None),
        P("expert", None, None),
        P("expert", "dp", None),
        P("expert", "dp", None),
        P("expert", "dp", None),
    )
    return jax.shard_map(
        body, mesh=mesh, in_specs=placed, out_specs=P("expert", "dp", None), check_vma=False
    )
```

profile of v0, /device:TPU:11, one launch (start us, length us, event | category | flops | bytes accessed | tf_op | source)
XLA Modules:
  0.0 349.2 jit_solution(17131210079808650329)
XLA Ops:
  6.5 0.0 copy-start
  6.5 0.9 copy.26
  7.5 0.1 eq.26
  7.5 0.1 squeeze.4
  7.6 0.7 broadcast_multiply_fusion
  8.3 1.2 reduce-window.6
  9.6 0.2 slice_reduce_fusion
  9.8 0.1 copy.31
  9.9 0.1 mul.70
  10.0 0.1 reshape.134
  10.1 0.1 fusion.42
  10.2 2.4 scatter_custom_fusion
  12.7 1.2 fusion.31
  14.0 0.1 broadcast_in_dim.43
  14.1 1.2 fusion.33
  15.3 0.9 concatenate.6
  16.2 16.2 %gather_fusion = bf16[1024,4096]{1,0:T(8,128)(2,1)} fusion(bf16[65,4096]{1,0:T(8,128)(2,1)} %concatenate.6, s32[1024]{0:T(1024)S(1)} %fusion.44), kind=kCustom, calls=%fused_computation | custom fusion | bytes 16781312 | tf_op jit(solution)/shard_map/jit(_take)/gather | solution.py:42
  32.4 7.4 %broadcast_select_fusion = bf16[32,2,16,4096]{3,2,1,0:T(8,128)(2,1)} fusion(bf16[32,2,16,4096]{3,2,1,0:T(8,128)(2,1)} %bitcast.77, pred[32,2,16]{2,1,0:T(4,128)(4,1)S(1)} %broadcast_in_dim.43), kind=kLoop, calls=%fused_computation.5 | loop fusion | flops 4194304 | bytes 16778240 | tf_op jit(solution)/shard_map/jit(_take)/select_n | solution.py:42
  39.8 0.0 copy-start.5
  39.9 102.1 %all_to_all.10 = bf16[32,2,16,4096]{3,2,1,0:T(8,128)(2,1)S(1)} all-to-all(bf16[32,2,16,4096]{3,2,1,0:T(8,128)(2,1)} %broadcast_select_fusion), channel_id=1, replica_groups=mesh['dp'=8,'expert'=32] {'expert'}, dimensions={0} | all-to-all | bytes 16777216 | tf_op jit(solution)/shard_map/all_to_all | solution.py:45
  141.9 0.0 copy-start.2
  141.9 3.2 copy-done.2
  145.1 0.0 copy-done.5
  145.1 3.3 fusion.7
  148.5 0.0 copy-done
  148.5 13.7 %convert_bitcast_fusion = bf16[32,2,16,4096]{3,2,0,1:T(8,128)(2,1)} fusion(bf16[2,192,4096]{2,1,0:T(8,128)(2,1)S(1)} %copy-done, bf16[2,192,4096]{2,1,0:T(8,128)(2,1)} %param.12, bf16[32,2,16,4096]{3,2,1,0:T(8,128)(2,1)} %copy-done.2, f32[32,2,16,192]{3,2,0,1:T(8,128)} %fusion.7), kind=kOutput, calls=%fused_computation.4 | convolution fusion | flops 3226599424 | bytes 23855104 | tf_op jit(solution)/shard_map/sjmf,jfd->sjmd/dot_general | solution.py:49
  162.2 7.7 %copy.34 = bf16[32,2,16,4096]{3,2,1,0:T(8,128)(2,1)} copy(bf16[32,2,16,4096]{3,2,0,1:T(8,128)(2,1)} %convert_bitcast_fusion) | data formatting | bytes 16777216 | tf_op jit(solution)/shard_map/convert_element_type | solution.py:51
  169.9 0.0 copy-start.3
  169.9 0.0 copy-start.4
  170.0 7.2 %all-to-all-start.1 = ((bf16[32,2,16,4096]{3,2,1,0:T(8,128)(2,1)}), bf16[32,2,16,4096]{3,2,1,0:T(8,128)(2,1)}, u32[]{:S(2)}, u32[]{:S(2)}) async-start(bf16[32,2,16,4096]{3,2,1,0:T(8,128)(2,1)} %copy.34), calls=%async_computation.1 | async-start | bytes 16777216 | tf_op jit(solution)/shard_map/all_to_all | solution.py:52
  177.1 0.0 reduce-scatter.2.cloned.1.call-start
  177.2 0.1 reduce_sum.32
  177.3 0.1 copy.29
  177.3 0.0 copy-done.3
  177.3 0.1 copy.30
  177.5 0.0 copy-done.4
  177.5 0.1 copy.35
  177.6 99.7 %all-to-all-done.1 = bf16[32,2,16,4096]{3,2,1,0:T(8,128)(2,1)} async-done(((bf16[32,2,16,4096]{3,2,1,0:T(8,128)(2,1)}), bf16[32,2,16,4096]{3,2,1,0:T(8,128)(2,1)}, u32[]{:S(2)}, u32[]{:S(2)}) %all-to-all-start.1) | async-done | bytes 8388640 | tf_op jit(solution)/shard_map/all_to_all | solution.py:52
  277.2 7.7 %concatenate.7 = bf16[1025,4096]{1,0:T(8,128)(2,1)} pad(bf16[1024,4096]{1,0:T(8,128)(2,1)} %bitcast.16, bf16[]{:T(256)} %constant.49.clone.1), padding=0_1x0_0 | pad | bytes 16785410 | tf_op jit(solution)/shard_map/concatenate | solution.py:53
  285.0 0.0 copy-start.1
  285.0 13.2 %gather_fusion.1 = bf16[512,4096]{1,0:T(8,128)(2,1)} fusion(bf16[1025,4096]{1,0:T(8,128)(2,1)} %concatenate.7, s32[1024]{0:T(1024)S(1)} %pad_clamp_fusion), kind=kCustom, calls=%fused_computation.1 | custom fusion | bytes 8390656 | tf_op jit(solution)/shard_map/jit(_take)/gather | solution.py:61
  298.2 7.9 %multiply_reduce_fusion = bf16[64,4096]{1,0:T(8,128)(2,1)} fusion(bf16[512,4096]{1,0:T(8,128)(2,1)} %gather_fusion.1, f32[64,8]{1,0:T(8,128)S(1)} %copy.35, pred[64,8]{1,0:T(8,128)(4,1)S(1)} %copy.30), kind=kLoop, calls=%fused_computation.3 | loop fusion | flops 8126464 | bytes 4721152 | tf_op jit(solution)/shard_map/reduce_sum | solution.py:66
  306.1 0.0 reduce-scatter.2.cloned.1.call-update
  306.1 36.2 %reduce-scatter.2.cloned.1.call-done = bf16[8,4096]{1,0:T(8,128)(2,1)} async-done(((bf16[64,4096]{1,0:T(8,128)(2,1)}), bf16[8,4096]{1,0:T(8,128)(2,1)}) %reduce-scatter.2.cloned.1.call-update) | async-done | bytes 65552 | tf_op jit(solution)/shard_map/reduce_scatter | solution.py:65
  342.3 0.0 copy-done.1
  (10 shorter events, 0.1 us)
Async XLA Ops:
  6.5 142.0 %copy-start = (bf16[2,192,4096]{2,1,0:T(8,128)(2,1)S(1)}, bf16[2,192,4096]{2,1,0:T(8,128)(2,1)}, u32[]{:S(2)}) copy-start(bf16[2,192,4096]{2,1,0:T(8,128)(2,1)} %param.13) | copy-start | bytes 9437188
  39.8 105.3 %copy-start.5 = (bf16[2,192,4096]{2,1,0:T(8,128)(2,1)S(1)}, bf16[2,192,4096]{2,1,0:T(8,128)(2,1)}, u32[]{:S(2)}) copy-start(bf16[2,192,4096]{2,1,0:T(8,128)(2,1)} %param.11) | copy-start | bytes 9437188
  141.9 3.2 copy-start.2
  169.9 7.4 %copy-start.3 = (s32[1,64,8]{1,2,0:T(8,128)S(1)}, s32[1,64,8]{1,2,0:T(8,128)}, u32[]{:S(2)}) copy-start(s32[1,64,8]{1,2,0:T(8,128)} %param.9) | copy-start | bytes 6148
  169.9 7.5 %copy-start.4 = (f32[1,64,8]{1,2,0:T(8,128)S(1)}, f32[1,64,8]{1,2,0:T(8,128)}, u32[]{:S(2)}) copy-start(f32[1,64,8]{1,2,0:T(8,128)} %param.10) | copy-start | bytes 6148
  170.0 107.3 %all-to-all-start.1 = ((bf16[32,2,16,4096]{3,2,1,0:T(8,128)(2,1)}), bf16[32,2,16,4096]{3,2,1,0:T(8,128)(2,1)}, u32[]{:S(2)}, u32[]{:S(2)}) async-start(bf16[32,2,16,4096]{3,2,1,0:T(8,128)(2,1)} %copy.34), calls=%async_computation.1 | async-start | bytes 16777216 | tf_op jit(solution)/shard_map/all_to_all | solution.py:52
  177.1 165.2 %reduce-scatter.2.cloned.1.call-start = ((), (), s32[]{:S(2)}) async-start(), calls=%async_computation.3 | async-start | bytes 589824 | tf_op jit(solution)/shard_map/reduce_scatter | solution.py:65
  285.0 57.3 %copy-start.1 = (bf16[2,192,4096]{2,1,0:T(8,128)(2,1)S(1)}, bf16[2,192,4096]{2,1,0:T(8,128)(2,1)}, u32[]{:S(2)}) copy-start(bf16[2,192,4096]{2,1,0:T(8,128)(2,1)} %param.13) | copy-start | bytes 9437188
Sparse Core Ops, SparseCore 0:
  306.2 36.0 reduce-scatter.1
where the time goes:
time: 354 us; the launch traced here: 349 us
  waiting for transfers between devices  136 us (38%)
  blocking collectives  102 us (29%)
  local copies, waits for them, and re-layouts  53.5 us (15%)
  other arithmetic  19.9 us (6%)
  matrix products  17.1 us (5%)
  between operations  13.5 us (4%)
  starting transfers between devices  7.21 us (2%)
    all_to_all x1, blocking collectives, body(): lax.all_to_all(outgoing, 'expert', split_axis=0, concat_axis=0, tiled=True)  102 us
    all_to_all x1, waiting for transfers between devices, body(): lax.all_to_all(partial_rows, 'expert', split_axis=0, concat_axis=0, tiled...  99.7 us
    reduce_scatter x1, waiting for transfers between devices, body(): lax.psum_scatter(jnp.sum(picked * group_weights[:, :, None], axis=1).asty...  36.2 us
    gather x1, local copies, waits for them, and re-layouts, body(): jnp.take(padded, sources, axis=0)  16.2 us
    dot_general x1, matrix products, body(): jnp.einsum('sjmf,jfd->sjmd', hidden, down_proj, preferred_element_type=jn...  13.7 us
    gather x1, local copies, waits for them, and re-layouts, body(): jnp.take(lookup, slot_index.reshape(-1), axis=0)  13.2 us
    reduce_sum x1, other arithmetic, body(): jnp.sum(picked * group_weights[:, :, None], axis=1).astype(jnp.bfloat16)  7.88 us
    concatenate x1, local copies, waits for them, and re-layouts, body(): jnp.concatenate([returned.reshape(experts * capacity, model_width), jnp.z...  7.73 us
  transfers between devices with their start and end apart: 2, of which 2 were waited for; matrix products, arithmetic and copies ran while one was open for 0% of the time, Pallas kernels for 0%

commit v1 on v0

--- a/solution.py
+++ b/solution.py
@@ -25,23 +25,18 @@
     top_k = group_ids.shape[1]
     experts = local_experts * expert_count
     capacity = dp_count * (group_size * top_k // (experts * dp_count) + 1)
+    slot_count = experts * capacity
     tok_float = tokens[0].astype(jnp.float32)
     inv_rms = lax.rsqrt(jnp.mean(tok_float * tok_float, axis=-1, keepdims=True) + 1e-06)
     group_rows = (tok_float * inv_rms * norm_gain).astype(jnp.bfloat16)
     slot_rank = rank_slots(group_ids, experts)
     slot_index = group_ids * capacity + slot_rank
-    token_order = jnp.broadcast_to(
-        jnp.arange(group_size, dtype=jnp.int32)[:, None], (group_size, top_k)
+    hit = slot_index[None, :, :] == jnp.arange(slot_count, dtype=jnp.int32)[:, None, None]
+    dispatch = jnp.any(hit, axis=2).astype(jnp.bfloat16)
+    outgoing = jnp.dot(dispatch, group_rows, preferred_element_type=jnp.float32).astype(
+        jnp.bfloat16
     )
-    sources = (
-        jnp.full((experts * capacity,), group_size, jnp.int32)
-        .at[slot_index.reshape(-1)]
-        .set(token_order.reshape(-1))
-    )
-    padded = jnp.concatenate([group_rows, jnp.zeros((1, model_width), jnp.bfloat16)], axis=0)
-    outgoing = jnp.take(padded, sources, axis=0).reshape(
-        expert_count, local_experts, capacity, model_width
-    )
+    outgoing = outgoing.reshape(expert_count, local_experts, capacity, model_width)
     incoming = lax.all_to_all(outgoing, "expert", split_axis=0, concat_axis=0, tiled=True)
     gate_act = jnp.einsum("sjmd,jfd->sjmf", incoming, gate_proj, preferred_element_type=jnp.float32)
     up_act = jnp.einsum("sjmd,jfd->sjmf", incoming, up_proj, preferred_element_type=jnp.float32)
@@ -50,24 +45,16 @@
         "sjmf,jfd->sjmd", hidden, down_proj, preferred_element_type=jnp.float32
     ).astype(jnp.bfloat16)
     returned = lax.all_to_all(partial_rows, "expert", split_axis=0, concat_axis=0, tiled=True)
-    lookup = jnp.concatenate(
-        [
-            returned.reshape(experts * capacity, model_width),
-            jnp.zeros((1, model_width), jnp.bfloat16),
-        ],
-        axis=0,
+    combine = jnp.sum(jnp.where(hit, group_weights[None, :, :], 0.0), axis=2)
+    mixed_rows = jnp.dot(
+        combine.T,
+        returned.reshape(slot_count, model_width).astype(jnp.float32),
+        precision=lax.Precision.HIGHEST,
+        preferred_element_type=jnp.float32,
     )
-    picked = (
-        jnp.take(lookup, slot_index.reshape(-1), axis=0)
-        .reshape(own_rows * lax.axis_size("dp"), top_k, model_width)
-        .astype(jnp.float32)
-    )
-    mixed = lax.psum_scatter(
-        jnp.sum(picked * group_weights[:, :, None], axis=1).astype(jnp.bfloat16),
-        "dp",
-        scatter_dimension=0,
-        tiled=True,
-    )
+    pieces = mixed_rows.astype(jnp.bfloat16).reshape(dp_count, own_rows, model_width)
+    gathered = lax.all_to_all(pieces, "dp", split_axis=0, concat_axis=0, tiled=True)
+    mixed = jnp.sum(gathered.astype(jnp.float32), axis=0).astype(jnp.bfloat16)
     return mixed[None]
 
 

time: 354 us -> 281 us (0.79); the launches traced: 349 us -> 281 us
  local copies, waits for them, and re-layouts: 53.5 us -> 12.6 us
  waiting for transfers between devices: 136 us -> 99.3 us
  blocking collectives: 102 us -> 128 us
  between operations: 13.5 us -> 0.1 us
  other arithmetic: 19.9 us -> 6.5 us
  matrix products: 17.1 us -> 27.4 us
    reduce_scatter x1 -> x0, waiting for transfers between devices: 36.2 us -> none  [body(): lax.psum_scatter(jnp.sum(picked * group_weights[:, :, None], axis=1).asty...]
    gather x2 -> x0, local copies, waits for them, and re-layouts: 29.4 us -> none  [the longest x1 16.2 us: body(): jnp.take(padded, sources, axis=0)]
    all_to_all x0 -> x1, blocking collectives: none -> 26.1 us  [body(): lax.all_to_all(pieces, 'dp', split_axis=0, concat_axis=0, tiled=True)]
    dot_general x0 -> x2, matrix products: none -> 10.3 us  [the longest x1 6.85 us: body(): jnp.dot(combine.T, returned.reshape(slot_count, model_width).astype(jnp.f...]
    concatenate x2 -> x0, local copies, waits for them, and re-layouts: 8.64 us -> none  [the longest x1 7.73 us: body(): jnp.concatenate([returned.reshape(experts * capacity, model_width), jnp.z...]
    select_n x2 -> x0, other arithmetic: 7.42 us -> none  [the longest x1 7.41 us: body(): jnp.take(padded, sources, axis=0)]
    reduce_sum x1 -> x2, other arithmetic: 7.88 us -> 2.47 us  [the longest x1 1.76 us: body(): mixed = jnp.sum(gathered.astype(jnp.float32), axis=0).astype(jnp.bfloat16)]
  transfers between devices with their start and end apart: 2 -> 1, of which waited for: 2 -> 1; matrix products, arithmetic and copies ran while one was open for 0% -> 0% of each run, Pallas kernels for 0% -> 0%
where the time goes in v1:
time: 281 us
  blocking collectives  128 us (46%)
  waiting for transfers between devices  99.3 us (35%)
  matrix products  27.4 us (10%)
  local copies, waits for them, and re-layouts  12.6 us (4%)
  starting transfers between devices  6.97 us (2%)
  other arithmetic  6.5 us (2%)
    all_to_all x1, blocking collectives, body(): lax.all_to_all(outgoing, 'expert', split_axis=0, concat_axis=0, tiled=True)  102 us
    all_to_all x1, waiting for transfers between devices, body(): lax.all_to_all(partial_rows, 'expert', split_axis=0, concat_axis=0, tiled...  99.3 us
    all_to_all x1, blocking collectives, body(): lax.all_to_all(pieces, 'dp', split_axis=0, concat_axis=0, tiled=True)  26.1 us
    dot_general x1, matrix products, body(): jnp.einsum('sjmf,jfd->sjmd', hidden, down_proj, preferred_element_type=jn...  13.7 us
    convert_element_type x1, local copies, waits for them, and re-layouts, body(): partial_rows = jnp.einsum('sjmf,jfd->sjmd', hidden, down_proj, preferred_...  7.7 us
    all_to_all x1, starting transfers between devices, body(): lax.all_to_all(partial_rows, 'expert', split_axis=0, concat_axis=0, tiled...  6.97 us
    dot_general x1, matrix products, body(): jnp.dot(combine.T, returned.reshape(slot_count, model_width).astype(jnp.f...  6.85 us
  transfers between devices with their start and end apart: 1, of which 1 were waited for; matrix products, arithmetic and copies ran while one was open for 0% of the time, Pallas kernels for 0%

profile of v1, /device:TPU:11, one launch (start us, length us, event | category | flops | bytes accessed | tf_op | source)
XLA Modules:
  0.0 280.8 jit_solution(16960080064823734447)
XLA Ops:
  0.0 0.0 copy-start
  0.0 0.9 copy.37
  0.9 0.1 eq.44
  1.0 0.1 eq.40
  1.1 1.2 reduce-window.6
  2.3 0.2 slice_reduce_fusion
  2.6 0.1 fusion.48
  2.7 0.1 reshape.42
  2.8 0.1 copy.40
  2.9 0.7 add_bitcast_fusion.1
  3.6 0.1 copy.41
  3.7 0.7 fusion.8
  4.4 1.2 fusion.33
  5.6 3.5 %convolution_convert_fusion = bf16[1024,4096]{1,0:T(8,128)(2,1)S(1)} fusion(pred[1024,64]{0,1:T(8,128)(4,1)S(1)} %fusion.8, bf16[1,64,4096]{2,1,0:T(8,128)(2,1)} %param.7, f32[4096]{0:T(1024)} %param.8, f32[64]{0:T(128)S(1)} %add_rsqrt_fusion), kind=kOutput, calls=%fused_computation.1 | convolution fusion | flops 542113792 | bytes 8995072 | tf_op jit(solution)/shard_map/dot_general | solution.py:36
  9.1 0.0 copy-start.3
  9.1 101.9 %all_to_all.15 = bf16[32,2,16,4096]{3,2,1,0:T(8,128)(2,1)S(1)} all-to-all(bf16[32,2,16,4096]{3,2,1,0:T(8,128)(2,1)S(1)} %bitcast.74), channel_id=1, replica_groups=mesh['dp'=8,'expert'=32] {'expert'}, dimensions={0} | all-to-all | bytes 16777216 | tf_op jit(solution)/shard_map/all_to_all | solution.py:40
  111.0 0.0 copy-start.1
  111.0 3.2 %copy-done.1 = bf16[32,2,16,4096]{3,2,1,0:T(8,128)(2,1)} copy-done((bf16[32,2,16,4096]{3,2,1,0:T(8,128)(2,1)}, bf16[32,2,16,4096]{3,2,1,0:T(8,128)(2,1)S(1)}, u32[]{:S(2)}) %copy-start.1) | copy-done | bytes 8388632
  114.2 0.0 copy-done.3
  114.2 3.3 %fusion.9 = f32[32,2,16,192]{3,2,0,1:T(8,128)} fusion(bf16[2,192,4096]{2,1,0:T(8,128)(2,1)S(1)} %copy-done.3, bf16[32,2,16,4096]{3,2,1,0:T(8,128)(2,1)S(1)} %all_to_all.15), kind=kOutput, calls=%fused_computation.14 | convolution fusion | flops 1610612736 | bytes 12320768 | tf_op jit(solution)/shard_map/sjmd,jfd->sjmf/dot_general | solution.py:41
  117.6 0.0 copy-done
  117.6 13.7 %convert_bitcast_fusion = bf16[32,2,16,4096]{3,2,0,1:T(8,128)(2,1)} fusion(bf16[2,192,4096]{2,1,0:T(8,128)(2,1)S(1)} %copy-done, bf16[2,192,4096]{2,1,0:T(8,128)(2,1)} %param.12, bf16[32,2,16,4096]{3,2,1,0:T(8,128)(2,1)} %copy-done.1, f32[32,2,16,192]{3,2,0,1:T(8,128)} %fusion.9), kind=kOutput, calls=%fused_computation | convolution fusion | flops 3226599424 | bytes 23855104 | tf_op jit(solution)/shard_map/sjmf,jfd->sjmd/dot_general | solution.py:44
  131.3 7.7 %copy.45 = bf16[32,2,16,4096]{3,2,1,0:T(8,128)(2,1)} copy(bf16[32,2,16,4096]{3,2,0,1:T(8,128)(2,1)} %convert_bitcast_fusion) | data formatting | bytes 16777216 | tf_op jit(solution)/shard_map/convert_element_type | solution.py:46
  139.0 0.0 copy-start.2
  139.0 7.0 %all-to-all-start.1 = ((bf16[32,2,16,4096]{3,2,1,0:T(8,128)(2,1)}), bf16[32,2,16,4096]{3,2,1,0:T(8,128)(2,1)}, u32[]{:S(2)}, u32[]{:S(2)}) async-start(bf16[32,2,16,4096]{3,2,1,0:T(8,128)(2,1)} %copy.45), calls=%async_computation.1 | async-start | bytes 16777216 | tf_op jit(solution)/shard_map/all_to_all | solution.py:47
  146.0 0.0 copy-done.2
  146.0 0.1 copy.42
  146.1 0.7 select_reduce_fusion
  146.8 99.3 %all-to-all-done.1 = bf16[32,2,16,4096]{3,2,1,0:T(8,128)(2,1)} async-done(((bf16[32,2,16,4096]{3,2,1,0:T(8,128)(2,1)}), bf16[32,2,16,4096]{3,2,1,0:T(8,128)(2,1)}, u32[]{:S(2)}, u32[]{:S(2)}) %all-to-all-start.1) | async-done | bytes 8388640 | tf_op jit(solution)/shard_map/all_to_all | solution.py:47
  246.1 6.8 %fusion.4 = bf16[8,8,4096]{2,1,0:T(8,128)(2,1)S(1)} fusion(f32[1024,64]{0,1:T(8,128)S(1)} %select_reduce_fusion, bf16[1024,4096]{1,0:T(8,128)(2,1)} %bitcast.15), kind=kOutput, calls=%fused_computation.7 | convolution fusion | flops 3221487616 | bytes 9175040 | tf_op jit(solution)/shard_map/dot_general | solution.py:49
  252.9 26.1 %all_to_all.16 = bf16[8,8,4096]{2,1,0:T(8,128)(2,1)} all-to-all(bf16[8,8,4096]{2,1,0:T(8,128)(2,1)S(1)} %fusion.4), channel_id=1, replica_groups=mesh['dp'=8,'expert'=32] {'dp'}, dimensions={0} | all-to-all | bytes 1048576 | tf_op jit(solution)/shard_map/all_to_all | solution.py:56
  279.1 1.8 reduce_sum.42
  (4 shorter events, 0.1 us)
Async XLA Ops:
  0.0 117.6 %copy-start = (bf16[2,192,4096]{2,1,0:T(8,128)(2,1)S(1)}, bf16[2,192,4096]{2,1,0:T(8,128)(2,1)}, u32[]{:S(2)}) copy-start(bf16[2,192,4096]{2,1,0:T(8,128)(2,1)} %param.13) | copy-start | bytes 9437188
  9.1 105.1 %copy-start.3 = (bf16[2,192,4096]{2,1,0:T(8,128)(2,1)S(1)}, bf16[2,192,4096]{2,1,0:T(8,128)(2,1)}, u32[]{:S(2)}) copy-start(bf16[2,192,4096]{2,1,0:T(8,128)(2,1)} %param.11) | copy-start | bytes 9437188
  111.0 3.2 %copy-start.1 = (bf16[32,2,16,4096]{3,2,1,0:T(8,128)(2,1)}, bf16[32,2,16,4096]{3,2,1,0:T(8,128)(2,1)S(1)}, u32[]{:S(2)}) copy-start(bf16[32,2,16,4096]{3,2,1,0:T(8,128)(2,1)S(1)} %all_to_all.15) | copy-start | bytes 25165828
  139.0 7.0 %copy-start.2 = (f32[1,64,8]{1,2,0:T(8,128)S(1)}, f32[1,64,8]{1,2,0:T(8,128)}, u32[]{:S(2)}) copy-start(f32[1,64,8]{1,2,0:T(8,128)} %param.10) | copy-start | bytes 6148
  139.0 107.1 %all-to-all-start.1 = ((bf16[32,2,16,4096]{3,2,1,0:T(8,128)(2,1)}), bf16[32,2,16,4096]{3,2,1,0:T(8,128)(2,1)}, u32[]{:S(2)}, u32[]{:S(2)}) async-start(bf16[32,2,16,4096]{3,2,1,0:T(8,128)(2,1)} %copy.45), calls=%async_computation.1 | async-start | bytes 16777216 | tf_op jit(solution)/shard_map/all_to_all | solution.py:47

commit v2 on v1

--- a/solution.py
+++ b/solution.py
@@ -38,20 +38,30 @@
     )
     outgoing = outgoing.reshape(expert_count, local_experts, capacity, model_width)
     incoming = lax.all_to_all(outgoing, "expert", split_axis=0, concat_axis=0, tiled=True)
-    gate_act = jnp.einsum("sjmd,jfd->sjmf", incoming, gate_proj, preferred_element_type=jnp.float32)
-    up_act = jnp.einsum("sjmd,jfd->sjmf", incoming, up_proj, preferred_element_type=jnp.float32)
-    hidden = (jax.nn.silu(gate_act) * up_act).astype(jnp.bfloat16)
-    partial_rows = jnp.einsum(
-        "sjmf,jfd->sjmd", hidden, down_proj, preferred_element_type=jnp.float32
+    rows = incoming.reshape(slot_count, model_width)
+    hidden_width = local_experts * gate_proj.shape[1]
+    gate_act = jnp.dot(
+        rows, gate_proj.reshape(hidden_width, model_width).T, preferred_element_type=jnp.float32
+    )
+    up_act = jnp.dot(
+        rows, up_proj.reshape(hidden_width, model_width).T, preferred_element_type=jnp.float32
+    )
+    row_expert = (jnp.arange(rows.shape[0], dtype=jnp.int32) // capacity) % local_experts
+    col_expert = jnp.arange(hidden_width, dtype=jnp.int32) // gate_proj.shape[1]
+    own_block = row_expert[:, None] == col_expert[None, :]
+    hidden = jnp.where(own_block, jax.nn.silu(gate_act) * up_act, 0.0).astype(jnp.bfloat16)
+    partial_rows = jnp.dot(
+        hidden, down_proj.reshape(hidden_width, model_width), preferred_element_type=jnp.float32
     ).astype(jnp.bfloat16)
+    partial_rows = partial_rows.reshape(expert_count, local_experts, capacity, model_width)
     returned = lax.all_to_all(partial_rows, "expert", split_axis=0, concat_axis=0, tiled=True)
     combine = jnp.sum(jnp.where(hit, group_weights[None, :, :], 0.0), axis=2)
+    combine_hi = combine.astype(jnp.bfloat16)
+    combine_lo = (combine - combine_hi.astype(jnp.float32)).astype(jnp.bfloat16)
+    flat_returned = returned.reshape(slot_count, model_width)
     mixed_rows = jnp.dot(
-        combine.T,
-        returned.reshape(slot_count, model_width).astype(jnp.float32),
-        precision=lax.Precision.HIGHEST,
-        preferred_element_type=jnp.float32,
-    )
+        combine_hi.T, flat_returned, preferred_element_type=jnp.float32
+    ) + jnp.dot(combine_lo.T, flat_returned, preferred_element_type=jnp.float32)
     pieces = mixed_rows.astype(jnp.bfloat16).reshape(dp_count, own_rows, model_width)
     gathered = lax.all_to_all(pieces, "dp", split_axis=0, concat_axis=0, tiled=True)
     mixed = jnp.sum(gathered.astype(jnp.float32), axis=0).astype(jnp.bfloat16)

time: 281 us -> 294 us (1.046)
  blocking collectives: 128 us -> 26.1 us
  waiting for transfers between devices: 99.3 us -> 199 us
  matrix products: 27.4 us -> 41.1 us
  starting transfers between devices: 6.97 us -> 18.7 us
  local copies, waits for them, and re-layouts: 12.6 us -> 1.66 us
    all_to_all x1 -> x0, blocking collectives: 102 us -> none  [body(): lax.all_to_all(outgoing, 'expert', split_axis=0, concat_axis=0, tiled=True)]
    all_to_all x0 -> x1, waiting for transfers between devices: none -> 100 us  [body(): lax.all_to_all(outgoing, 'expert', split_axis=0, concat_axis=0, tiled=True)]
    dot_general x3 -> x4, matrix products: 23.9 us -> 34.4 us  [the longest x1 14.6 us: body(): jnp.dot(hidden, down_proj.reshape(hidden_width, model_width), preferred_e...]
    all_to_all x0 -> x1, starting transfers between devices: none -> 7.88 us  [body(): lax.all_to_all(outgoing, 'expert', split_axis=0, concat_axis=0, tiled=True)]
    convert_element_type x1 -> x0, local copies, waits for them, and re-layouts: 7.7 us -> none  [body(): partial_rows = jnp.einsum('sjmf,jfd->sjmd', hidden, down_proj, preferred_...]
    all_to_all x1, starting transfers between devices: 6.97 us -> 10.8 us  [body(): lax.all_to_all(partial_rows, 'expert', split_axis=0, concat_axis=0, tiled...]
    dot_general x1, matrix products: 3.46 us -> 6.67 us  [body(): jnp.dot(dispatch, group_rows, preferred_element_type=jnp.float32)]
    unnamed x9 -> x5, local copies, waits for them, and re-layouts: 4.14 us -> 0.93 us
  transfers between devices with their start and end apart: 1 -> 2, of which waited for: 1 -> 2; matrix products, arithmetic and copies ran while one was open for 0% -> 0% of each run, Pallas kernels for 0% -> 0%
where the time goes in v2:
time: 294 us
  waiting for transfers between devices  199 us (68%)
  matrix products  41.1 us (14%)
  blocking collectives  26.1 us (9%)
  starting transfers between devices  18.7 us (6%)
  other arithmetic  6.51 us (2%)
    all_to_all x1, waiting for transfers between devices, body(): lax.all_to_all(outgoing, 'expert', split_axis=0, concat_axis=0, tiled=True)  100 us
    all_to_all x1, waiting for transfers between devices, body(): lax.all_to_all(partial_rows, 'expert', split_axis=0, concat_axis=0, tiled...  99.3 us
    all_to_all x1, blocking collectives, body(): lax.all_to_all(pieces, 'dp', split_axis=0, concat_axis=0, tiled=True)  26.1 us
    dot_general x1, matrix products, body(): jnp.dot(hidden, down_proj.reshape(hidden_width, model_width), preferred_e...  14.6 us
    all_to_all x1, starting transfers between devices, body(): lax.all_to_all(partial_rows, 'expert', split_axis=0, concat_axis=0, tiled...  10.8 us
    dot_general x1, matrix products, body(): jnp.dot(rows, gate_proj.reshape(hidden_width, model_width).T, preferred_e...  9.94 us
    all_to_all x1, starting transfers between devices, body(): lax.all_to_all(outgoing, 'expert', split_axis=0, concat_axis=0, tiled=True)  7.88 us
    dot_general x1, matrix products, body(): jnp.dot(dispatch, group_rows, preferred_element_type=jnp.float32)  6.67 us
  transfers between devices with their start and end apart: 2, of which 2 were waited for; matrix products, arithmetic and copies ran while one was open for 0% of the time, Pallas kernels for 0%

profile of v2, /device:TPU:11, one launch (start us, length us, event | category | flops | bytes accessed | tf_op | source)
XLA Modules:
  0.0 293.6 jit_solution(10765271881195983424)
XLA Ops:
  0.0 0.0 copy-start
  0.0 0.9 copy.22
  0.9 0.1 eq.59
  1.0 0.1 eq.55
  1.1 1.2 reduce-window.6
  2.3 0.2 slice_reduce_fusion
  2.6 0.1 fusion.12
  2.7 0.1 reshape.94
  2.8 0.1 copy.25
  2.9 0.7 add_bitcast_fusion.1
  3.6 0.1 copy.26
  3.7 0.7 fusion.2
  4.4 1.2 fusion.3
  5.6 6.7 %convolution_convert_fusion.1 = bf16[1024,4096]{1,0:T(8,128)(2,1)} fusion(pred[1024,64]{0,1:T(8,128)(4,1)S(1)} %fusion.2, bf16[1,64,4096]{2,1,0:T(8,128)(2,1)} %param.7, f32[4096]{0:T(1024)} %param.8, f32[64]{0:T(128)S(1)} %add_rsqrt_fusion), kind=kOutput, calls=%fused_computation.1 | convolution fusion | flops 542113792 | bytes 8995072 | tf_op jit(solution)/shard_map/dot_general | solution.py:36
  12.3 7.9 %all-to-all-start = ((bf16[32,2,16,4096]{3,2,1,0:T(8,128)(2,1)}), bf16[32,2,16,4096]{3,2,1,0:T(8,128)(2,1)}, u32[]{:S(2)}, u32[]{:S(2)}) async-start(bf16[32,2,16,4096]{3,2,1,0:T(8,128)(2,1)} %bitcast.48), calls=%async_computation | async-start | bytes 16777216 | tf_op jit(solution)/shard_map/all_to_all | solution.py:40
  20.2 100.1 %all-to-all-done = bf16[32,2,16,4096]{3,2,1,0:T(8,128)(2,1)} async-done(((bf16[32,2,16,4096]{3,2,1,0:T(8,128)(2,1)}), bf16[32,2,16,4096]{3,2,1,0:T(8,128)(2,1)}, u32[]{:S(2)}, u32[]{:S(2)}) %all-to-all-start) | async-done | bytes 8388640 | tf_op jit(solution)/shard_map/all_to_all | solution.py:40
  120.3 9.9 %fusion.26 = f32[1024,384]{1,0:T(8,128)} fusion(bf16[1024,4096]{1,0:T(8,128)(2,1)} %bitcast.6, bf16[384,4096]{1,0:T(8,128)(2,1)} %bitcast.51), kind=kOutput, calls=%fused_computation.52 | convolution fusion | flops 3221225472 | bytes 13107200 | tf_op jit(solution)/shard_map/dot_general | solution.py:43
  130.2 0.0 copy-done
  130.2 14.6 %convolution_convert_fusion = bf16[1024,4096]{1,0:T(8,128)(2,1)} fusion(bf16[384,4096]{1,0:T(8,128)(2,1)S(1)} %bitcast.47, f32[1024,384]{1,0:T(8,128)} %fusion.26, bf16[1024,4096]{1,0:T(8,128)(2,1)} %bitcast.6, bf16[384,4096]{1,0:T(8,128)(2,1)} %bitcast.52, s32[384]{0:T(512)S(1)} %add_select_fusion.2, s32[1024]{0:T(1024)S(1)} %add_select_fusion), kind=kOutput, calls=%fused_computation | convolution fusion | flops 6449790976 | bytes 24647168 | tf_op jit(solution)/shard_map/dot_general | solution.py:53
  144.8 0.0 copy-start.1
  144.8 10.8 %all-to-all-start.1 = ((bf16[32,2,16,4096]{3,2,1,0:T(8,128)(2,1)}), bf16[32,2,16,4096]{3,2,1,0:T(8,128)(2,1)}, u32[]{:S(2)}, u32[]{:S(2)}) async-start(bf16[32,2,16,4096]{3,2,1,0:T(8,128)(2,1)} %bitcast.49), calls=%async_computation.1 | async-start | bytes 16777216 | tf_op jit(solution)/shard_map/all_to_all | solution.py:57
  155.6 0.0 copy-done.1
  155.6 0.1 copy.27
  155.7 0.7 select_reduce_fusion
  156.4 99.3 %all-to-all-done.1 = bf16[32,2,16,4096]{3,2,1,0:T(8,128)(2,1)} async-done(((bf16[32,2,16,4096]{3,2,1,0:T(8,128)(2,1)}), bf16[32,2,16,4096]{3,2,1,0:T(8,128)(2,1)}, u32[]{:S(2)}, u32[]{:S(2)}) %all-to-all-start.1) | async-done | bytes 8388640 | tf_op jit(solution)/shard_map/all_to_all | solution.py:57
  255.7 4.9 %fusion.15 = f32[64,4096]{1,0:T(8,128)S(1)} fusion(bf16[1024,4096]{1,0:T(8,128)(2,1)} %bitcast.11, f32[1024,64]{0,1:T(8,128)S(1)} %select_reduce_fusion), kind=kOutput, calls=%fused_computation.28 | convolution fusion | flops 536936448 | bytes 9699328 | tf_op jit(solution)/shard_map/dot_general | solution.py:62
  260.7 5.0 %fusion.1 = bf16[8,8,4096]{2,1,0:T(8,128)(2,1)S(1)} fusion(f32[64,4096]{1,0:T(8,128)S(1)} %fusion.15, bf16[1024,4096]{1,0:T(8,128)(2,1)} %bitcast.11, f32[1024,64]{0,1:T(8,128)S(1)} %select_reduce_fusion), kind=kOutput, calls=%fused_computation.4 | convolution fusion | flops 537657344 | bytes 10223616 | tf_op jit(solution)/shard_map/dot_general | solution.py:64
  265.7 26.1 %all_to_all.15 = bf16[8,8,4096]{2,1,0:T(8,128)(2,1)} all-to-all(bf16[8,8,4096]{2,1,0:T(8,128)(2,1)S(1)} %fusion.1), channel_id=1, replica_groups=mesh['dp'=8,'expert'=32] {'dp'}, dimensions={0} | all-to-all | bytes 1048576 | tf_op jit(solution)/shard_map/all_to_all | solution.py:66
  291.8 1.8 reduce_sum.42
  (6 shorter events, 0.1 us)
Async XLA Ops:
  0.0 130.2 %copy-start = (bf16[2,192,4096]{2,1,0:T(8,128)(2,1)S(1)}, bf16[2,192,4096]{2,1,0:T(8,128)(2,1)}, u32[]{:S(2)}) copy-start(bf16[2,192,4096]{2,1,0:T(8,128)(2,1)} %param.13) | copy-start | bytes 9437188
  12.3 108.0 %all-to-all-start = ((bf16[32,2,16,4096]{3,2,1,0:T(8,128)(2,1)}), bf16[32,2,16,4096]{3,2,1,0:T(8,128)(2,1)}, u32[]{:S(2)}, u32[]{:S(2)}) async-start(bf16[32,2,16,4096]{3,2,1,0:T(8,128)(2,1)} %bitcast.48), calls=%async_computation | async-start | bytes 16777216 | tf_op jit(solution)/shard_map/all_to_all | solution.py:40
  144.8 10.8 %copy-start.1 = (f32[1,64,8]{1,2,0:T(8,128)S(1)}, f32[1,64,8]{1,2,0:T(8,128)}, u32[]{:S(2)}) copy-start(f32[1,64,8]{1,2,0:T(8,128)} %param.10) | copy-start | bytes 6148
  144.8 110.9 %all-to-all-start.1 = ((bf16[32,2,16,4096]{3,2,1,0:T(8,128)(2,1)}), bf16[32,2,16,4096]{3,2,1,0:T(8,128)(2,1)}, u32[]{:S(2)}, u32[]{:S(2)}) async-start(bf16[32,2,16,4096]{3,2,1,0:T(8,128)(2,1)} %bitcast.49), calls=%async_computation.1 | async-start | bytes 16777216 | tf_op jit(solution)/shard_map/all_to_all | solution.py:57

commit v3 on v1

--- a/solution.py
+++ b/solution.py
@@ -1,6 +1,7 @@
 import jax
 import jax.numpy as jnp
 from jax import lax
+from jax.experimental import pallas as pl
 from jax.sharding import PartitionSpec as P
 
 
@@ -11,6 +12,38 @@
     )
     before = jnp.cumsum(onehot, axis=0) - onehot
     return jnp.sum(before * onehot, axis=1).reshape(id_table.shape)
+
+
+def ffn_block(x_ref, gate_ref, up_ref, down_ref, out_ref):
+    width = x_ref.shape[3]
+    rows = x_ref[...].reshape(x_ref.shape[0] * x_ref.shape[2], width)
+    contract = (((1,), (1,)), ((), ()))
+    gate_act = lax.dot_general(rows, gate_ref[0], contract, preferred_element_type=jnp.float32)
+    up_act = lax.dot_general(rows, up_ref[0], contract, preferred_element_type=jnp.float32)
+    hidden = (gate_act / (1.0 + jnp.exp(-gate_act)) * up_act).astype(jnp.bfloat16)
+    partial = jnp.dot(hidden, down_ref[0], preferred_element_type=jnp.float32)
+    out_ref[...] = partial.astype(out_ref.dtype).reshape(out_ref.shape)
+
+
+def expert_ffn(incoming, gate_proj, up_proj, down_proj):
+    sources, local_experts, capacity, width = incoming.shape
+    hidden_width = gate_proj.shape[1]
+    per_step = 8
+    row_spec = pl.BlockSpec((per_step, 1, capacity, width), lambda j, b: (b, j, 0, 0))
+    weight_spec = pl.BlockSpec((1, hidden_width, width), lambda j, b: (j, 0, 0))
+    rows = sources * local_experts * capacity
+    return pl.pallas_call(
+        ffn_block,
+        grid=(local_experts, sources // per_step),
+        in_specs=[row_spec, weight_spec, weight_spec, weight_spec],
+        out_specs=row_spec,
+        out_shape=jax.ShapeDtypeStruct(incoming.shape, jnp.bfloat16),
+        cost_estimate=pl.CostEstimate(
+            flops=6 * rows * hidden_width * width,
+            transcendentals=rows * hidden_width,
+            bytes_accessed=4 * rows * width + 6 * local_experts * hidden_width * width,
+        ),
+    )(incoming, gate_proj, up_proj, down_proj)
 
 
 def body(tokens, norm_gain, expert_ids, route_weights, gate_proj, up_proj, down_proj):
@@ -38,12 +71,7 @@
     )
     outgoing = outgoing.reshape(expert_count, local_experts, capacity, model_width)
     incoming = lax.all_to_all(outgoing, "expert", split_axis=0, concat_axis=0, tiled=True)
-    gate_act = jnp.einsum("sjmd,jfd->sjmf", incoming, gate_proj, preferred_element_type=jnp.float32)
-    up_act = jnp.einsum("sjmd,jfd->sjmf", incoming, up_proj, preferred_element_type=jnp.float32)
-    hidden = (jax.nn.silu(gate_act) * up_act).astype(jnp.bfloat16)
-    partial_rows = jnp.einsum(
-        "sjmf,jfd->sjmd", hidden, down_proj, preferred_element_type=jnp.float32
-    ).astype(jnp.bfloat16)
+    partial_rows = expert_ffn(incoming, gate_proj, up_proj, down_proj)
     returned = lax.all_to_all(partial_rows, "expert", split_axis=0, concat_axis=0, tiled=True)
     combine = jnp.sum(jnp.where(hit, group_weights[None, :, :], 0.0), axis=2)
     mixed_rows = jnp.dot(

time: 281 us -> 270 us (0.961)
  Pallas kernels: 0 us -> 18.3 us
  matrix products: 27.4 us -> 10.3 us
  local copies, waits for them, and re-layouts: 12.6 us -> 1.51 us
    pallas_call x0 -> x1, Pallas kernels: none -> 18.3 us  [expert_ffn(): pl.pallas_call(ffn_block, grid=(local_experts, sources // per_step), in_s...]
    dot_general x2 -> x0, matrix products: 17.1 us -> none  [the longest x1 13.7 us: body(): jnp.einsum('sjmf,jfd->sjmd', hidden, down_proj, preferred_element_type=jn...]
    convert_element_type x1 -> x0, local copies, waits for them, and re-layouts: 7.7 us -> none  [body(): partial_rows = jnp.einsum('sjmf,jfd->sjmd', hidden, down_proj, preferred_...]
    unnamed x9 -> x3, local copies, waits for them, and re-layouts: 4.14 us -> 0.77 us
where the time goes in v3:
time: 270 us
  blocking collectives  128 us (47%)
  waiting for transfers between devices  99.3 us (37%)
  Pallas kernels  18.3 us (7%)
  matrix products  10.3 us (4%)
  starting transfers between devices  6.97 us (3%)
  other arithmetic  5.44 us (2%)
    all_to_all x1, blocking collectives, body(): lax.all_to_all(outgoing, 'expert', split_axis=0, concat_axis=0, tiled=True)  102 us
    all_to_all x1, waiting for transfers between devices, body(): lax.all_to_all(partial_rows, 'expert', split_axis=0, concat_axis=0, tiled...  99.3 us
    all_to_all x1, blocking collectives, body(): lax.all_to_all(pieces, 'dp', split_axis=0, concat_axis=0, tiled=True)  26.1 us
    pallas_call x1, Pallas kernels, expert_ffn(): pl.pallas_call(ffn_block, grid=(local_experts, sources // per_step), in_s...  18.3 us
    all_to_all x1, starting transfers between devices, body(): lax.all_to_all(partial_rows, 'expert', split_axis=0, concat_axis=0, tiled...  6.97 us
    dot_general x1, matrix products, body(): jnp.dot(combine.T, returned.reshape(slot_count, model_width).astype(jnp.f...  6.85 us
  transfers between devices with their start and end apart: 1, of which 1 were waited for; matrix products, arithmetic and copies ran while one was open for 0% of the time, Pallas kernels for 0%

profile of v3, /device:TPU:11, one launch (start us, length us, event | category | flops | bytes accessed | tf_op | source)
XLA Modules:
  0.0 269.6 jit_solution(14612079504482873360)
XLA Ops:
  0.0 0.8 copy.22
  0.8 0.1 eq.44
  0.9 0.1 eq.40
  1.0 1.2 reduce-window.6
  2.2 0.2 slice_reduce_fusion
  2.4 0.1 fusion.11
  2.6 0.1 reshape.42
  2.7 0.1 copy.25
  2.7 0.7 add_bitcast_fusion.1
  3.4 0.1 copy.26
  3.5 0.7 fusion.1
  4.2 1.2 fusion.2
  5.5 3.5 %convolution_convert_fusion = bf16[1024,4096]{1,0:T(8,128)(2,1)S(1)} fusion(pred[1024,64]{0,1:T(8,128)(4,1)S(1)} %fusion.1, bf16[1,64,4096]{2,1,0:T(8,128)(2,1)} %param.7, f32[4096]{0:T(1024)} %param.8, f32[64]{0:T(128)S(1)} %add_rsqrt_fusion), kind=kOutput, calls=%fused_computation | convolution fusion | flops 542113792 | bytes 8995072 | tf_op jit(solution)/shard_map/dot_general | solution.py:69
  9.0 101.7 %all_to_all.15.x_ref = bf16[32,2,16,4096]{3,2,1,0:T(8,128)(2,1)} all-to-all(bf16[32,2,16,4096]{3,2,1,0:T(8,128)(2,1)S(1)} %bitcast.37), channel_id=1, replica_groups=mesh['dp'=8,'expert'=32] {'expert'}, dimensions={0} | all-to-all | bytes 16777216 | tf_op jit(solution)/shard_map/all_to_all | solution.py:73
  110.7 18.3 %shard_map.73 = bf16[32,2,16,4096]{3,2,1,0:T(8,128)(2,1)} custom-call(bf16[32,2,16,4096]{3,2,1,0:T(8,128)(2,1)} %all_to_all.15.x_ref, bf16[2,192,4096]{2,1,0:T(8,128)(2,1)} %gate_ref.1, bf16[2,192,4096]{2,1,0:T(8,128)(2,1)} %up_ref.1, bf16[2,192,4096]{2,1,0:T(8,128)(2,1)} %down_ref.1), custom_call_target="tpu_custom_call" | custom-call | flops 4831838208 | bytes 26214400 | tf_op jit(solution)/shard_map/pallas_call | solution.py:35
  128.9 0.0 copy-start
  128.9 7.0 %all-to-all-start.1 = ((bf16[32,2,16,4096]{3,2,1,0:T(8,128)(2,1)}), bf16[32,2,16,4096]{3,2,1,0:T(8,128)(2,1)}, u32[]{:S(2)}, u32[]{:S(2)}) async-start(bf16[32,2,16,4096]{3,2,1,0:T(8,128)(2,1)} %shard_map.73), calls=%async_computation.1 | async-start | bytes 16777216 | tf_op jit(solution)/shard_map/all_to_all | solution.py:75
  135.9 0.0 copy-done
  135.9 0.1 copy.27
  136.0 0.7 select_reduce_fusion
  136.7 99.3 %all-to-all-done.1 = bf16[32,2,16,4096]{3,2,1,0:T(8,128)(2,1)} async-done(((bf16[32,2,16,4096]{3,2,1,0:T(8,128)(2,1)}), bf16[32,2,16,4096]{3,2,1,0:T(8,128)(2,1)}, u32[]{:S(2)}, u32[]{:S(2)}) %all-to-all-start.1) | async-done | bytes 8388640 | tf_op jit(solution)/shard_map/all_to_all | solution.py:75
  236.0 6.8 %fusion = bf16[8,8,4096]{2,1,0:T(8,128)(2,1)S(1)} fusion(f32[1024,64]{0,1:T(8,128)S(1)} %select_reduce_fusion, bf16[1024,4096]{1,0:T(8,128)(2,1)} %bitcast.6), kind=kOutput, calls=%fused_computation.2 | convolution fusion | flops 3221487616 | bytes 9175040 | tf_op jit(solution)/shard_map/dot_general | solution.py:77
  242.9 26.1 %all_to_all.16 = bf16[8,8,4096]{2,1,0:T(8,128)(2,1)S(1)} all-to-all(bf16[8,8,4096]{2,1,0:T(8,128)(2,1)S(1)} %fusion), channel_id=1, replica_groups=mesh['dp'=8,'expert'=32] {'dp'}, dimensions={0} | all-to-all | bytes 1048576 | tf_op jit(solution)/shard_map/all_to_all | solution.py:84
  268.9 0.7 reduce_sum.42
  (4 shorter events, 0.1 us)
Async XLA Ops:
  128.9 7.0 %copy-start = (f32[1,64,8]{1,2,0:T(8,128)S(1)}, f32[1,64,8]{1,2,0:T(8,128)}, u32[]{:S(2)}) copy-start(f32[1,64,8]{1,2,0:T(8,128)} %param.10) | copy-start | bytes 6148
  128.9 107.1 %all-to-all-start.1 = ((bf16[32,2,16,4096]{3,2,1,0:T(8,128)(2,1)}), bf16[32,2,16,4096]{3,2,1,0:T(8,128)(2,1)}, u32[]{:S(2)}, u32[]{:S(2)}) async-start(bf16[32,2,16,4096]{3,2,1,0:T(8,128)(2,1)} %shard_map.73), calls=%async_computation.1 | async-start | bytes 16777216 | tf_op jit(solution)/shard_map/all_to_all | solution.py:75

commit v4 on v3

--- a/solution.py
+++ b/solution.py
@@ -70,10 +70,11 @@
         jnp.bfloat16
     )
     outgoing = outgoing.reshape(expert_count, local_experts, capacity, model_width)
+    combine = jnp.sum(jnp.where(hit, group_weights[None, :, :], 0.0), axis=2)
+    combine, outgoing = lax.optimization_barrier((combine, outgoing))
     incoming = lax.all_to_all(outgoing, "expert", split_axis=0, concat_axis=0, tiled=True)
     partial_rows = expert_ffn(incoming, gate_proj, up_proj, down_proj)
     returned = lax.all_to_all(partial_rows, "expert", split_axis=0, concat_axis=0, tiled=True)
-    combine = jnp.sum(jnp.where(hit, group_weights[None, :, :], 0.0), axis=2)
     mixed_rows = jnp.dot(
         combine.T,
         returned.reshape(slot_count, model_width).astype(jnp.float32),

time: 270 us -> 264 us (0.978)
  blocking collectives: 128 us -> 228 us
  waiting for transfers between devices: 99.3 us -> 0 us
  starting transfers between devices: 6.97 us -> 0 us
    all_to_all x0 -> x1, blocking collectives: none -> 101 us  [body(): lax.all_to_all(partial_rows, 'expert', split_axis=0, concat_axis=0, tiled...]
    all_to_all x1 -> x0, waiting for transfers between devices: 99.3 us -> none  [body(): lax.all_to_all(partial_rows, 'expert', split_axis=0, concat_axis=0, tiled...]
    all_to_all x1 -> x0, starting transfers between devices: 6.97 us -> none  [body(): lax.all_to_all(partial_rows, 'expert', split_axis=0, concat_axis=0, tiled...]
  transfers between devices with their start and end apart: 1 -> 0, of which waited for: 1 -> 0; matrix products, arithmetic and copies ran while one was open for 0% -> 0% of each run, Pallas kernels for 0% -> 0%
where the time goes in v4:
time: 264 us; the launch traced here: 262 us
  blocking collectives  228 us (86%)
  Pallas kernels  18.3 us (7%)
  matrix products  7.93 us (3%)
  other arithmetic  5.45 us (2%)
    all_to_all x1, blocking collectives, body(): lax.all_to_all(outgoing, 'expert', split_axis=0, concat_axis=0, tiled=True)  102 us
    all_to_all x1, blocking collectives, body(): lax.all_to_all(partial_rows, 'expert', split_axis=0, concat_axis=0, tiled...  101 us
    all_to_all x1, blocking collectives, body(): lax.all_to_all(pieces, 'dp', split_axis=0, concat_axis=0, tiled=True)  25.8 us
    pallas_call x1, Pallas kernels, expert_ffn(): pl.pallas_call(ffn_block, grid=(local_experts, sources // per_step), in_s...  18.3 us

profile of v4, /device:TPU:11, one launch (start us, length us, event | category | flops | bytes accessed | tf_op | source)
XLA Modules:
  0.0 262.1 jit_solution(10838108293564762491)
XLA Ops:
  0.0 0.8 copy.22
  0.8 0.1 eq.44
  0.9 0.1 eq.40
  1.0 1.2 fusion.2
  2.2 0.8 copy.27
  3.0 1.2 reduce-window.6
  4.2 0.2 slice_reduce_fusion
  4.5 0.1 fusion.11
  4.6 0.1 reshape.42
  4.7 0.1 copy.25
  4.8 0.7 add_bitcast_fusion.1
  5.5 0.1 copy.26
  5.6 0.7 fusion.1
  6.3 0.7 select_reduce_fusion
  7.0 3.5 %convolution_convert_fusion = bf16[1024,4096]{1,0:T(8,128)(2,1)S(1)} fusion(pred[1024,64]{0,1:T(8,128)(4,1)S(1)} %fusion.1, bf16[1,64,4096]{2,1,0:T(8,128)(2,1)} %param.7, f32[4096]{0:T(1024)} %param.8, f32[64]{0:T(128)S(1)} %add_rsqrt_fusion), kind=kOutput, calls=%fused_computation | convolution fusion | flops 542113792 | bytes 8995072 | tf_op jit(solution)/shard_map/dot_general | solution.py:69
  10.5 101.7 %all_to_all.15.x_ref = bf16[32,2,16,4096]{3,2,1,0:T(8,128)(2,1)} all-to-all(bf16[32,2,16,4096]{3,2,1,0:T(8,128)(2,1)S(1)} %bitcast.38), channel_id=1, replica_groups=mesh['dp'=8,'expert'=32] {'expert'}, dimensions={0} | all-to-all | bytes 16777216 | tf_op jit(solution)/shard_map/all_to_all | solution.py:75
  112.2 18.3 %shard_map.73 = bf16[32,2,16,4096]{3,2,1,0:T(8,128)(2,1)} custom-call(bf16[32,2,16,4096]{3,2,1,0:T(8,128)(2,1)} %all_to_all.15.x_ref, bf16[2,192,4096]{2,1,0:T(8,128)(2,1)} %gate_ref.1, bf16[2,192,4096]{2,1,0:T(8,128)(2,1)} %up_ref.1, bf16[2,192,4096]{2,1,0:T(8,128)(2,1)} %down_ref.1), custom_call_target="tpu_custom_call" | custom-call | flops 4831838208 | bytes 26214400 | tf_op jit(solution)/shard_map/pallas_call | solution.py:35
  130.4 100.7 %all_to_all.16 = bf16[32,2,16,4096]{3,2,1,0:T(8,128)(2,1)S(1)} all-to-all(bf16[32,2,16,4096]{3,2,1,0:T(8,128)(2,1)} %shard_map.73), channel_id=1, replica_groups=mesh['dp'=8,'expert'=32] {'expert'}, dimensions={0} | all-to-all | bytes 16777216 | tf_op jit(solution)/shard_map/all_to_all | solution.py:77
  231.1 4.5 %fusion = bf16[8,8,4096]{2,1,0:T(8,128)(2,1)S(1)} fusion(f32[1024,64]{0,1:T(8,128)S(1)} %select_reduce_fusion, bf16[1024,4096]{1,0:T(8,128)(2,1)S(1)} %bitcast.37), kind=kOutput, calls=%fused_computation.2 | convolution fusion | flops 3221487616 | bytes 9175040 | tf_op jit(solution)/shard_map/dot_general | solution.py:78
  235.6 25.8 %all_to_all.17 = bf16[8,8,4096]{2,1,0:T(8,128)(2,1)S(1)} all-to-all(bf16[8,8,4096]{2,1,0:T(8,128)(2,1)S(1)} %fusion), channel_id=1, replica_groups=mesh['dp'=8,'expert'=32] {'dp'}, dimensions={0} | all-to-all | bytes 1048576 | tf_op jit(solution)/shard_map/all_to_all | solution.py:85
  261.4 0.7 reduce_sum.42
  (4 shorter events, 0.1 us)

commit v5 on v4

--- a/solution.py
+++ b/solution.py
@@ -28,7 +28,7 @@
 def expert_ffn(incoming, gate_proj, up_proj, down_proj):
     sources, local_experts, capacity, width = incoming.shape
     hidden_width = gate_proj.shape[1]
-    per_step = 8
+    per_step = 16
     row_spec = pl.BlockSpec((per_step, 1, capacity, width), lambda j, b: (b, j, 0, 0))
     weight_spec = pl.BlockSpec((1, hidden_width, width), lambda j, b: (j, 0, 0))
     rows = sources * local_experts * capacity

time: 264 us -> 260 us (0.985)
  Pallas kernels: 18.3 us -> 14.6 us
    pallas_call x1, Pallas kernels: 18.3 us -> 14.6 us  [expert_ffn(): pl.pallas_call(ffn_block, grid=(local_experts, sources // per_step), in_s...]
where the time goes in v5:
time: 260 us; the launch traced here: 258 us
  blocking collectives  228 us (88%)
  Pallas kernels  14.6 us (6%)
  matrix products  7.94 us (3%)
  other arithmetic  5.45 us (2%)
    all_to_all x1, blocking collectives, body(): lax.all_to_all(outgoing, 'expert', split_axis=0, concat_axis=0, tiled=True)  102 us
    all_to_all x1, blocking collectives, body(): lax.all_to_all(partial_rows, 'expert', split_axis=0, concat_axis=0, tiled...  101 us
    all_to_all x1, blocking collectives, body(): lax.all_to_all(pieces, 'dp', split_axis=0, concat_axis=0, tiled=True)  25.8 us
    pallas_call x1, Pallas kernels, expert_ffn(): pl.pallas_call(ffn_block, grid=(local_experts, sources // per_step), in_s...  14.6 us

profile of v5, /device:TPU:11, one launch (start us, length us, event | category | flops | bytes accessed | tf_op | source)
XLA Modules:
  0.0 258.4 jit_solution(13864523480899712076)
XLA Ops:
  0.0 0.8 copy.22
  0.8 0.1 eq.44
  0.9 0.1 eq.40
  1.0 1.2 fusion.2
  2.2 0.8 copy.27
  3.0 1.2 reduce-window.6
  4.2 0.2 slice_reduce_fusion
  4.5 0.1 fusion.11
  4.6 0.1 reshape.42
  4.7 0.1 copy.25
  4.8 0.7 add_bitcast_fusion.1
  5.5 0.1 copy.26
  5.6 0.7 fusion.1
  6.3 0.7 select_reduce_fusion
  7.0 3.5 %convolution_convert_fusion = bf16[1024,4096]{1,0:T(8,128)(2,1)S(1)} fusion(pred[1024,64]{0,1:T(8,128)(4,1)S(1)} %fusion.1, bf16[1,64,4096]{2,1,0:T(8,128)(2,1)} %param.7, f32[4096]{0:T(1024)} %param.8, f32[64]{0:T(128)S(1)} %add_rsqrt_fusion), kind=kOutput, calls=%fused_computation | convolution fusion | flops 542113792 | bytes 8995072 | tf_op jit(solution)/shard_map/dot_general | solution.py:69
  10.5 101.7 %all_to_all.15.x_ref = bf16[32,2,16,4096]{3,2,1,0:T(8,128)(2,1)} all-to-all(bf16[32,2,16,4096]{3,2,1,0:T(8,128)(2,1)S(1)} %bitcast.38), channel_id=1, replica_groups=mesh['dp'=8,'expert'=32] {'expert'}, dimensions={0} | all-to-all | bytes 16777216 | tf_op jit(solution)/shard_map/all_to_all | solution.py:75
  112.2 14.6 %shard_map.73 = bf16[32,2,16,4096]{3,2,1,0:T(8,128)(2,1)} custom-call(bf16[32,2,16,4096]{3,2,1,0:T(8,128)(2,1)} %all_to_all.15.x_ref, bf16[2,192,4096]{2,1,0:T(8,128)(2,1)} %gate_ref.1, bf16[2,192,4096]{2,1,0:T(8,128)(2,1)} %up_ref.1, bf16[2,192,4096]{2,1,0:T(8,128)(2,1)} %down_ref.1), custom_call_target="tpu_custom_call" | custom-call | flops 4831838208 | bytes 26214400 | tf_op jit(solution)/shard_map/pallas_call | solution.py:35
  126.8 100.7 %all_to_all.16 = bf16[32,2,16,4096]{3,2,1,0:T(8,128)(2,1)S(1)} all-to-all(bf16[32,2,16,4096]{3,2,1,0:T(8,128)(2,1)} %shard_map.73), channel_id=1, replica_groups=mesh['dp'=8,'expert'=32] {'expert'}, dimensions={0} | all-to-all | bytes 16777216 | tf_op jit(solution)/shard_map/all_to_all | solution.py:77
  227.5 4.5 %fusion = bf16[8,8,4096]{2,1,0:T(8,128)(2,1)S(1)} fusion(f32[1024,64]{0,1:T(8,128)S(1)} %select_reduce_fusion, bf16[1024,4096]{1,0:T(8,128)(2,1)S(1)} %bitcast.37), kind=kOutput, calls=%fused_computation.2 | convolution fusion | flops 3221487616 | bytes 9175040 | tf_op jit(solution)/shard_map/dot_general | solution.py:78
  232.0 25.8 %all_to_all.17 = bf16[8,8,4096]{2,1,0:T(8,128)(2,1)S(1)} all-to-all(bf16[8,8,4096]{2,1,0:T(8,128)(2,1)S(1)} %fusion), channel_id=1, replica_groups=mesh['dp'=8,'expert'=32] {'dp'}, dimensions={0} | all-to-all | bytes 1048576 | tf_op jit(solution)/shard_map/all_to_all | solution.py:85
  257.7 0.7 reduce_sum.42
  (4 shorter events, 0.1 us)

commit v6 on v5

--- a/solution.py
+++ b/solution.py
@@ -71,6 +71,8 @@
     )
     outgoing = outgoing.reshape(expert_count, local_experts, capacity, model_width)
     combine = jnp.sum(jnp.where(hit, group_weights[None, :, :], 0.0), axis=2)
+    place = lax.axis_index("dp")
+    combine = jnp.roll(combine, -own_rows * place, axis=1)
     combine, outgoing = lax.optimization_barrier((combine, outgoing))
     incoming = lax.all_to_all(outgoing, "expert", split_axis=0, concat_axis=0, tiled=True)
     partial_rows = expert_ffn(incoming, gate_proj, up_proj, down_proj)
@@ -82,8 +84,13 @@
         preferred_element_type=jnp.float32,
     )
     pieces = mixed_rows.astype(jnp.bfloat16).reshape(dp_count, own_rows, model_width)
-    gathered = lax.all_to_all(pieces, "dp", split_axis=0, concat_axis=0, tiled=True)
-    mixed = jnp.sum(gathered.astype(jnp.float32), axis=0).astype(jnp.bfloat16)
+    total = pieces[0].astype(jnp.float32)
+    for shift in range(1, dp_count):
+        inbound = lax.ppermute(
+            pieces[shift], "dp", [(i, (i + shift) % dp_count) for i in range(dp_count)]
+        )
+        total = total + inbound.astype(jnp.float32)
+    mixed = total.astype(jnp.bfloat16)
     return mixed[None]
 
 

time: 260 us -> 260 us (level)
  blocking collectives: 228 us -> 202 us
  starting transfers between devices: 0 us -> 16.5 us
  waiting for transfers between devices: 0 us -> 7.74 us
    all_to_all x1 -> x0, blocking collectives: 25.8 us -> none  [body(): lax.all_to_all(pieces, 'dp', split_axis=0, concat_axis=0, tiled=True)]
    ppermute x0 -> x7, starting transfers between devices: none -> 16.5 us  [body(): lax.ppermute(pieces[shift], 'dp', [(i, (i + shift) % dp_count) for i in r...]
    ppermute x0 -> x7, waiting for transfers between devices: none -> 7.74 us  [body(): lax.ppermute(pieces[shift], 'dp', [(i, (i + shift) % dp_count) for i in r...]
  transfers between devices with their start and end apart: 0 -> 7, of which waited for: 0 -> 2; matrix products, arithmetic and copies ran while one was open for 0% -> 0% of each run, Pallas kernels for 0% -> 0%
where the time goes in v6:
time: 260 us; the launch traced here: 257 us
  blocking collectives  202 us (78%)
  starting transfers between devices  16.5 us (6%)
  Pallas kernels  14.6 us (6%)
  matrix products  7.93 us (3%)
  waiting for transfers between devices  7.74 us (3%)
  other arithmetic  5.5 us (2%)
    all_to_all x1, blocking collectives, body(): lax.all_to_all(outgoing, 'expert', split_axis=0, concat_axis=0, tiled=True)  102 us
    all_to_all x1, blocking collectives, body(): lax.all_to_all(partial_rows, 'expert', split_axis=0, concat_axis=0, tiled...  101 us
    ppermute x7, starting transfers between devices, body(): lax.ppermute(pieces[shift], 'dp', [(i, (i + shift) % dp_count) for i in r...  16.5 us
    pallas_call x1, Pallas kernels, expert_ffn(): pl.pallas_call(ffn_block, grid=(local_experts, sources // per_step), in_s...  14.6 us
    ppermute x7, waiting for transfers between devices, body(): lax.ppermute(pieces[shift], 'dp', [(i, (i + shift) % dp_count) for i in r...  7.74 us
  transfers between devices with their start and end apart: 7, of which 2 were waited for; matrix products, arithmetic and copies ran while one was open for 0% of the time, Pallas kernels for 0%

profile of v6, /device:TPU:11, one launch (start us, length us, event | category | flops | bytes accessed | tf_op | source)
XLA Modules:
  0.0 257.1 jit_solution(8150374363756836038)
XLA Ops:
  0.0 0.8 copy.22
  0.8 0.1 eq.47
  0.9 0.1 eq.43
  1.0 1.2 fusion.1
  2.2 0.8 copy.27
  3.0 1.2 reduce-window.6
  4.2 0.2 slice_reduce_fusion
  4.5 0.1 fusion.11
  4.6 0.1 reshape.56
  4.7 0.1 copy.25
  4.8 0.7 add_bitcast_fusion.1
  5.5 0.1 copy.26
  5.6 0.7 fusion
  6.3 0.7 select_reduce_fusion
  7.0 0.1 fusion.8
  7.1 3.5 %convolution_convert_fusion = bf16[1024,4096]{1,0:T(8,128)(2,1)S(1)} fusion(pred[1024,64]{0,1:T(8,128)(4,1)S(1)} %fusion, bf16[1,64,4096]{2,1,0:T(8,128)(2,1)} %param.7, f32[4096]{0:T(1024)} %param.8, f32[64]{0:T(128)S(1)} %add_rsqrt_fusion), kind=kOutput, calls=%fused_computation | convolution fusion | flops 542113792 | bytes 8995072 | tf_op jit(solution)/shard_map/dot_general | solution.py:69
  10.5 101.7 %all_to_all.10.x_ref = bf16[32,2,16,4096]{3,2,1,0:T(8,128)(2,1)} all-to-all(bf16[32,2,16,4096]{3,2,1,0:T(8,128)(2,1)S(1)} %bitcast.37), channel_id=1, replica_groups=mesh['dp'=8,'expert'=32] {'expert'}, dimensions={0} | all-to-all | bytes 16777216 | tf_op jit(solution)/shard_map/all_to_all | solution.py:77
  112.3 14.6 %shard_map.73 = bf16[32,2,16,4096]{3,2,1,0:T(8,128)(2,1)} custom-call(bf16[32,2,16,4096]{3,2,1,0:T(8,128)(2,1)} %all_to_all.10.x_ref, bf16[2,192,4096]{2,1,0:T(8,128)(2,1)} %gate_ref.1, bf16[2,192,4096]{2,1,0:T(8,128)(2,1)} %up_ref.1, bf16[2,192,4096]{2,1,0:T(8,128)(2,1)} %down_ref.1), custom_call_target="tpu_custom_call" | custom-call | flops 4831838208 | bytes 26214400 | tf_op jit(solution)/shard_map/pallas_call | solution.py:35
  126.8 100.7 %all_to_all.11 = bf16[32,2,16,4096]{3,2,1,0:T(8,128)(2,1)S(1)} all-to-all(bf16[32,2,16,4096]{3,2,1,0:T(8,128)(2,1)} %shard_map.73), channel_id=1, replica_groups=mesh['dp'=8,'expert'=32] {'expert'}, dimensions={0} | all-to-all | bytes 16777216 | tf_op jit(solution)/shard_map/all_to_all | solution.py:79
  227.6 4.5 %convolution_convert_fusion.1 = bf16[64,4096]{1,0:T(8,128)(2,1)S(1)} fusion(f32[1024,64]{0,1:T(8,128)S(1)} %fusion.8, bf16[1024,4096]{1,0:T(8,128)(2,1)S(1)} %bitcast.36), kind=kOutput, calls=%fused_computation.1 | convolution fusion | flops 3221487616 | bytes 9175040 | tf_op jit(solution)/shard_map/dot_general | solution.py:80
  232.1 1.7 collective-permute-start
  233.8 4.0 %collective-permute-start.6 = (bf16[8,4096]{1,0:T(8,128)(2,1)S(1)}, bf16[8,4096]{1,0:T(8,128)(2,1)S(1)}, u32[]{:S(2)}, u32[]{:S(2)}) collective-permute-start(bf16[8,4096]{1,0:T(8,128)(2,1)S(1)} %get-tuple-element.10), channel_id=1, source_target_pairs={{0,224},{32,0},{64,32},{96,64},{128,96},{160,128},{192,160},{224,1... | collective-permute-start | bytes 196616 | tf_op jit(solution)/shard_map/ppermute | solution.py:89
  237.8 1.8 collective-permute-start.5
  239.7 2.1 collective-permute-start.4
  241.8 2.8 %collective-permute-start.3 = (bf16[8,4096]{1,0:T(8,128)(2,1)S(1)}, bf16[8,4096]{1,0:T(8,128)(2,1)S(1)}, u32[]{:S(2)}, u32[]{:S(2)}) collective-permute-start(bf16[8,4096]{1,0:T(8,128)(2,1)S(1)} %get-tuple-element.13), channel_id=1, source_target_pairs={{0,128},{32,160},{64,192},{96,224},{128,0},{160,32},{192,64},{224,... | collective-permute-start | bytes 196616 | tf_op jit(solution)/shard_map/ppermute | solution.py:89
  244.6 0.0 collective-permute-done
  244.6 0.4 collective-permute-start.2
  245.0 0.0 collective-permute-done.6
  245.1 3.6 %collective-permute-start.1 = (bf16[8,4096]{1,0:T(8,128)(2,1)S(1)}, bf16[8,4096]{1,0:T(8,128)(2,1)S(1)}, u32[]{:S(2)}, u32[]{:S(2)}) collective-permute-start(bf16[8,4096]{1,0:T(8,128)(2,1)S(1)} %get-tuple-element.15), channel_id=1, source_target_pairs={{0,64},{32,96},{64,128},{96,160},{128,192},{160,224},{192,0},{224,... | collective-permute-start | bytes 196616 | tf_op jit(solution)/shard_map/ppermute | solution.py:89
  248.6 0.0 collective-permute-done.5
  248.6 0.0 collective-permute-done.4
  248.6 2.5 collective-permute-done.3
  251.2 5.2 %collective-permute-done.2 = bf16[8,4096]{1,0:T(8,128)(2,1)S(1)} collective-permute-done((bf16[8,4096]{1,0:T(8,128)(2,1)S(1)}, bf16[8,4096]{1,0:T(8,128)(2,1)S(1)}, u32[]{:S(2)}, u32[]{:S(2)}) %collective-permute-start.2) | collective-permute-done | bytes 65568 | tf_op jit(solution)/shard_map/ppermute | solution.py:89
  256.4 0.0 collective-permute-done.1
  256.4 0.7 fusion.13
  (5 shorter events, 0.1 us)
Async XLA Ops:
  232.1 12.5 %collective-permute-start = (bf16[8,4096]{1,0:T(8,128)(2,1)S(1)}, bf16[8,4096]{1,0:T(8,128)(2,1)S(1)}, u32[]{:S(2)}, u32[]{:S(2)}) collective-permute-start(bf16[8,4096]{1,0:T(8,128)(2,1)S(1)} %get-tuple-element.9), channel_id=1, source_target_pairs={{0,32},{32,64},{64,96},{96,128},{128,160},{160,192},{192,224},{224... | collective-permute-start | bytes 196616 | tf_op jit(solution)/shard_map/ppermute | solution.py:89
  233.8 11.2 %collective-permute-start.6 = (bf16[8,4096]{1,0:T(8,128)(2,1)S(1)}, bf16[8,4096]{1,0:T(8,128)(2,1)S(1)}, u32[]{:S(2)}, u32[]{:S(2)}) collective-permute-start(bf16[8,4096]{1,0:T(8,128)(2,1)S(1)} %get-tuple-element.10), channel_id=1, source_target_pairs={{0,224},{32,0},{64,32},{96,64},{128,96},{160,128},{192,160},{224,1... | collective-permute-start | bytes 196616 | tf_op jit(solution)/shard_map/ppermute | solution.py:89
  237.8 10.8 %collective-permute-start.5 = (bf16[8,4096]{1,0:T(8,128)(2,1)S(1)}, bf16[8,4096]{1,0:T(8,128)(2,1)S(1)}, u32[]{:S(2)}, u32[]{:S(2)}) collective-permute-start(bf16[8,4096]{1,0:T(8,128)(2,1)S(1)} %get-tuple-element.11), channel_id=1, source_target_pairs={{0,192},{32,224},{64,0},{96,32},{128,64},{160,96},{192,128},{224,1... | collective-permute-start | bytes 196616 | tf_op jit(solution)/shard_map/ppermute | solution.py:89
  239.7 9.0 %collective-permute-start.4 = (bf16[8,4096]{1,0:T(8,128)(2,1)S(1)}, bf16[8,4096]{1,0:T(8,128)(2,1)S(1)}, u32[]{:S(2)}, u32[]{:S(2)}) collective-permute-start(bf16[8,4096]{1,0:T(8,128)(2,1)S(1)} %get-tuple-element.12), channel_id=1, source_target_pairs={{0,160},{32,192},{64,224},{96,0},{128,32},{160,64},{192,96},{224,1... | collective-permute-start | bytes 196616 | tf_op jit(solution)/shard_map/ppermute | solution.py:89
  241.8 9.4 %collective-permute-start.3 = (bf16[8,4096]{1,0:T(8,128)(2,1)S(1)}, bf16[8,4096]{1,0:T(8,128)(2,1)S(1)}, u32[]{:S(2)}, u32[]{:S(2)}) collective-permute-start(bf16[8,4096]{1,0:T(8,128)(2,1)S(1)} %get-tuple-element.13), channel_id=1, source_target_pairs={{0,128},{32,160},{64,192},{96,224},{128,0},{160,32},{192,64},{224,... | collective-permute-start | bytes 196616 | tf_op jit(solution)/shard_map/ppermute | solution.py:89
  244.6 11.8 %collective-permute-start.2 = (bf16[8,4096]{1,0:T(8,128)(2,1)S(1)}, bf16[8,4096]{1,0:T(8,128)(2,1)S(1)}, u32[]{:S(2)}, u32[]{:S(2)}) collective-permute-start(bf16[8,4096]{1,0:T(8,128)(2,1)S(1)} %get-tuple-element.14), channel_id=1, source_target_pairs={{0,96},{32,128},{64,160},{96,192},{128,224},{160,0},{192,32},{224,... | collective-permute-start | bytes 196616 | tf_op jit(solution)/shard_map/ppermute | solution.py:89
  245.1 11.3 %collective-permute-start.1 = (bf16[8,4096]{1,0:T(8,128)(2,1)S(1)}, bf16[8,4096]{1,0:T(8,128)(2,1)S(1)}, u32[]{:S(2)}, u32[]{:S(2)}) collective-permute-start(bf16[8,4096]{1,0:T(8,128)(2,1)S(1)} %get-tuple-element.15), channel_id=1, source_target_pairs={{0,64},{32,96},{64,128},{96,160},{128,192},{160,224},{192,0},{224,... | collective-permute-start | bytes 196616 | tf_op jit(solution)/shard_map/ppermute | solution.py:89

commit v7 on v5

--- a/solution.py
+++ b/solution.py
@@ -28,7 +28,7 @@
 def expert_ffn(incoming, gate_proj, up_proj, down_proj):
     sources, local_experts, capacity, width = incoming.shape
     hidden_width = gate_proj.shape[1]
-    per_step = 16
+    per_step = 32
     row_spec = pl.BlockSpec((per_step, 1, capacity, width), lambda j, b: (b, j, 0, 0))
     weight_spec = pl.BlockSpec((1, hidden_width, width), lambda j, b: (j, 0, 0))
     rows = sources * local_experts * capacity

time: 260 us -> 258 us (level)
  no operation moved by 1% of the time
where the time goes in v7:
time: 258 us; the launch traced here: 256 us
  blocking collectives  228 us (88%)
  Pallas kernels  12.4 us (5%)
  matrix products  7.94 us (3%)
  other arithmetic  5.45 us (2%)
    all_to_all x1, blocking collectives, body(): lax.all_to_all(outgoing, 'expert', split_axis=0, concat_axis=0, tiled=True)  102 us
    all_to_all x1, blocking collectives, body(): lax.all_to_all(partial_rows, 'expert', split_axis=0, concat_axis=0, tiled...  101 us
    all_to_all x1, blocking collectives, body(): lax.all_to_all(pieces, 'dp', split_axis=0, concat_axis=0, tiled=True)  25.8 us
    pallas_call x1, Pallas kernels, expert_ffn(): pl.pallas_call(ffn_block, grid=(local_experts, sources // per_step), in_s...  12.4 us

profile of v7, /device:TPU:11, one launch (start us, length us, event | category | flops | bytes accessed | tf_op | source)
XLA Modules:
  0.0 256.3 jit_solution(9509780849159759351)
XLA Ops:
  0.0 0.8 copy.22
  0.8 0.1 eq.44
  0.9 0.1 eq.40
  1.0 1.2 fusion.2
  2.2 0.8 copy.27
  3.0 1.2 reduce-window.6
  4.2 0.2 slice_reduce_fusion
  4.5 0.1 fusion.11
  4.6 0.1 reshape.42
  4.7 0.1 copy.25
  4.8 0.7 add_bitcast_fusion.1
  5.5 0.1 copy.26
  5.6 0.7 fusion.1
  6.3 0.7 select_reduce_fusion
  7.0 3.5 %convolution_convert_fusion = bf16[1024,4096]{1,0:T(8,128)(2,1)S(1)} fusion(pred[1024,64]{0,1:T(8,128)(4,1)S(1)} %fusion.1, bf16[1,64,4096]{2,1,0:T(8,128)(2,1)} %param.7, f32[4096]{0:T(1024)} %param.8, f32[64]{0:T(128)S(1)} %add_rsqrt_fusion), kind=kOutput, calls=%fused_computation | convolution fusion | flops 542113792 | bytes 8995072 | tf_op jit(solution)/shard_map/dot_general | solution.py:69
  10.5 101.7 %all_to_all.15.x_ref = bf16[32,2,16,4096]{3,2,1,0:T(8,128)(2,1)} all-to-all(bf16[32,2,16,4096]{3,2,1,0:T(8,128)(2,1)S(1)} %bitcast.38), channel_id=1, replica_groups=mesh['dp'=8,'expert'=32] {'expert'}, dimensions={0} | all-to-all | bytes 16777216 | tf_op jit(solution)/shard_map/all_to_all | solution.py:75
  112.2 12.4 %shard_map.73 = bf16[32,2,16,4096]{3,2,1,0:T(8,128)(2,1)} custom-call(bf16[32,2,16,4096]{3,2,1,0:T(8,128)(2,1)} %all_to_all.15.x_ref, bf16[2,192,4096]{2,1,0:T(8,128)(2,1)} %gate_ref.1, bf16[2,192,4096]{2,1,0:T(8,128)(2,1)} %up_ref.1, bf16[2,192,4096]{2,1,0:T(8,128)(2,1)} %down_ref.1), custom_call_target="tpu_custom_call" | custom-call | flops 4831838208 | bytes 26214400 | tf_op jit(solution)/shard_map/pallas_call | solution.py:35
  124.6 100.7 %all_to_all.16 = bf16[32,2,16,4096]{3,2,1,0:T(8,128)(2,1)S(1)} all-to-all(bf16[32,2,16,4096]{3,2,1,0:T(8,128)(2,1)} %shard_map.73), channel_id=1, replica_groups=mesh['dp'=8,'expert'=32] {'expert'}, dimensions={0} | all-to-all | bytes 16777216 | tf_op jit(solution)/shard_map/all_to_all | solution.py:77
  225.3 4.5 %fusion = bf16[8,8,4096]{2,1,0:T(8,128)(2,1)S(1)} fusion(f32[1024,64]{0,1:T(8,128)S(1)} %select_reduce_fusion, bf16[1024,4096]{1,0:T(8,128)(2,1)S(1)} %bitcast.37), kind=kOutput, calls=%fused_computation.2 | convolution fusion | flops 3221487616 | bytes 9175040 | tf_op jit(solution)/shard_map/dot_general | solution.py:78
  229.8 25.8 %all_to_all.17 = bf16[8,8,4096]{2,1,0:T(8,128)(2,1)S(1)} all-to-all(bf16[8,8,4096]{2,1,0:T(8,128)(2,1)S(1)} %fusion), channel_id=1, replica_groups=mesh['dp'=8,'expert'=32] {'dp'}, dimensions={0} | all-to-all | bytes 1048576 | tf_op jit(solution)/shard_map/all_to_all | solution.py:85
  255.6 0.7 reduce_sum.42
  (4 shorter events, 0.1 us)

commit v8 on v7

--- a/solution.py
+++ b/solution.py
@@ -71,16 +71,17 @@
     )
     outgoing = outgoing.reshape(expert_count, local_experts, capacity, model_width)
     combine = jnp.sum(jnp.where(hit, group_weights[None, :, :], 0.0), axis=2)
-    combine, outgoing = lax.optimization_barrier((combine, outgoing))
+    combine_hi = combine.astype(jnp.bfloat16)
+    combine_lo = (combine - combine_hi.astype(jnp.float32)).astype(jnp.bfloat16)
+    stacked = jnp.concatenate([combine_hi, combine_lo], axis=1)
+    stacked, outgoing = lax.optimization_barrier((stacked, outgoing))
     incoming = lax.all_to_all(outgoing, "expert", split_axis=0, concat_axis=0, tiled=True)
     partial_rows = expert_ffn(incoming, gate_proj, up_proj, down_proj)
     returned = lax.all_to_all(partial_rows, "expert", split_axis=0, concat_axis=0, tiled=True)
-    mixed_rows = jnp.dot(
-        combine.T,
-        returned.reshape(slot_count, model_width).astype(jnp.float32),
-        precision=lax.Precision.HIGHEST,
-        preferred_element_type=jnp.float32,
+    both_parts = jnp.dot(
+        stacked.T, returned.reshape(slot_count, model_width), preferred_element_type=jnp.float32
     )
+    mixed_rows = both_parts[:group_size] + both_parts[group_size:]
     pieces = mixed_rows.astype(jnp.bfloat16).reshape(dp_count, own_rows, model_width)
     gathered = lax.all_to_all(pieces, "dp", split_axis=0, concat_axis=0, tiled=True)
     mixed = jnp.sum(gathered.astype(jnp.float32), axis=0).astype(jnp.bfloat16)

time: 258 us -> 255 us (0.988)
  matrix products: 7.94 us -> 4.41 us
    dot_general x1, matrix products: 4.48 us -> 1.29 us  [body(): jnp.dot(stacked.T, returned.reshape(slot_count, model_width), preferred_e...]
where the time goes in v8:
time: 255 us; the launch traced here: 253 us
  blocking collectives  228 us (89%)
  Pallas kernels  12.4 us (5%)
  other arithmetic  5.59 us (2%)
  matrix products  4.41 us (2%)
    all_to_all x1, blocking collectives, body(): lax.all_to_all(outgoing, 'expert', split_axis=0, concat_axis=0, tiled=True)  102 us
    all_to_all x1, blocking collectives, body(): lax.all_to_all(partial_rows, 'expert', split_axis=0, concat_axis=0, tiled...  101 us
    all_to_all x1, blocking collectives, body(): lax.all_to_all(pieces, 'dp', split_axis=0, concat_axis=0, tiled=True)  25.8 us
    pallas_call x1, Pallas kernels, expert_ffn(): pl.pallas_call(ffn_block, grid=(local_experts, sources // per_step), in_s...  12.4 us

profile of v8, /device:TPU:11, one launch (start us, length us, event | category | flops | bytes accessed | tf_op | source)
XLA Modules:
  0.0 253.0 jit_solution(17769513968217596473)
XLA Ops:
  0.0 0.0 copy-start
  0.0 0.8 copy.22
  0.8 0.1 eq.44
  0.9 0.1 eq.40
  1.0 1.2 fusion.1
  2.3 0.8 copy.27
  3.1 1.2 reduce-window.6
  4.3 0.2 slice_reduce_fusion
  4.5 0.1 fusion.12
  4.7 0.1 reshape.42
  4.8 0.1 copy.25
  4.8 0.7 add_bitcast_fusion.1
  5.5 0.1 copy.26
  5.6 0.7 fusion
  6.3 0.7 select_reduce_fusion
  7.1 0.0 copy-done
  7.1 3.1 %convolution_convert_fusion = bf16[1024,4096]{1,0:T(8,128)(2,1)S(1)} fusion(pred[1024,64]{0,1:T(8,128)(4,1)S(1)} %fusion, bf16[1,64,4096]{2,1,0:T(8,128)(2,1)S(1)} %copy-done, f32[4096]{0:T(1024)} %param.8, f32[64]{0:T(128)S(1)} %add_rsqrt_fusion), kind=kOutput, calls=%fused_computation | convolution fusion | flops 542113792 | bytes 8995072 | tf_op jit(solution)/shard_map/dot_general | solution.py:69
  10.3 101.7 %all_to_all.15.x_ref = bf16[32,2,16,4096]{3,2,1,0:T(8,128)(2,1)} all-to-all(bf16[32,2,16,4096]{3,2,1,0:T(8,128)(2,1)S(1)} %bitcast.37), channel_id=1, replica_groups=mesh['dp'=8,'expert'=32] {'expert'}, dimensions={0} | all-to-all | bytes 16777216 | tf_op jit(solution)/shard_map/all_to_all | solution.py:78
  112.0 12.4 %shard_map.73 = bf16[32,2,16,4096]{3,2,1,0:T(8,128)(2,1)} custom-call(bf16[32,2,16,4096]{3,2,1,0:T(8,128)(2,1)} %all_to_all.15.x_ref, bf16[2,192,4096]{2,1,0:T(8,128)(2,1)} %gate_ref.1, bf16[2,192,4096]{2,1,0:T(8,128)(2,1)} %up_ref.1, bf16[2,192,4096]{2,1,0:T(8,128)(2,1)} %down_ref.1), custom_call_target="tpu_custom_call" | custom-call | flops 4831838208 | bytes 26214400 | tf_op jit(solution)/shard_map/pallas_call | solution.py:35
  124.4 100.7 %all_to_all.16 = bf16[32,2,16,4096]{3,2,1,0:T(8,128)(2,1)S(1)} all-to-all(bf16[32,2,16,4096]{3,2,1,0:T(8,128)(2,1)} %shard_map.73), channel_id=1, replica_groups=mesh['dp'=8,'expert'=32] {'expert'}, dimensions={0} | all-to-all | bytes 16777216 | tf_op jit(solution)/shard_map/all_to_all | solution.py:80
  225.1 1.3 fusion.14
  226.4 0.1 fusion.5
  226.5 25.8 %all_to_all.17 = bf16[8,8,4096]{2,1,0:T(8,128)(2,1)S(1)} all-to-all(bf16[8,8,4096]{2,1,0:T(8,128)(2,1)S(1)} %fusion.5), channel_id=1, replica_groups=mesh['dp'=8,'expert'=32] {'dp'}, dimensions={0} | all-to-all | bytes 1048576 | tf_op jit(solution)/shard_map/all_to_all | solution.py:86
  252.3 0.7 reduce_sum.42
  (6 shorter events, 0.1 us)
Async XLA Ops:
  0.0 7.1 %copy-start = (bf16[1,64,4096]{2,1,0:T(8,128)(2,1)S(1)}, bf16[1,64,4096]{2,1,0:T(8,128)(2,1)}, u32[]{:S(2)}) copy-start(bf16[1,64,4096]{2,1,0:T(8,128)(2,1)} %param.7) | copy-start | bytes 1572868

commit v9 on v8

--- a/solution.py
+++ b/solution.py
@@ -3,15 +3,6 @@
 from jax import lax
 from jax.experimental import pallas as pl
 from jax.sharding import PartitionSpec as P
-
-
-def rank_slots(id_table, expert_total):
-    flat_ids = id_table.reshape(-1)
-    onehot = (flat_ids[:, None] == jnp.arange(expert_total, dtype=jnp.int32)[None, :]).astype(
-        jnp.int32
-    )
-    before = jnp.cumsum(onehot, axis=0) - onehot
-    return jnp.sum(before * onehot, axis=1).reshape(id_table.shape)
 
 
 def ffn_block(x_ref, gate_ref, up_ref, down_ref, out_ref):
@@ -62,15 +53,24 @@
     tok_float = tokens[0].astype(jnp.float32)
     inv_rms = lax.rsqrt(jnp.mean(tok_float * tok_float, axis=-1, keepdims=True) + 1e-06)
     group_rows = (tok_float * inv_rms * norm_gain).astype(jnp.bfloat16)
-    slot_rank = rank_slots(group_ids, experts)
-    slot_index = group_ids * capacity + slot_rank
-    hit = slot_index[None, :, :] == jnp.arange(slot_count, dtype=jnp.int32)[:, None, None]
-    dispatch = jnp.any(hit, axis=2).astype(jnp.bfloat16)
+    chosen = group_ids[:, :, None] == jnp.arange(experts, dtype=jnp.int32)[None, None, :]
+    picks = jnp.any(chosen, axis=1)
+    weight_of = jnp.sum(jnp.where(chosen, group_weights[:, :, None], 0.0), axis=1)
+    token_at = jnp.arange(group_size, dtype=jnp.int32)
+    earlier = (token_at[:, None] > token_at[None, :]).astype(jnp.bfloat16)
+    rank = jnp.dot(earlier, picks.astype(jnp.bfloat16), preferred_element_type=jnp.float32)
+    place_hit = picks[:, :, None] & (
+        rank.astype(jnp.int32)[:, :, None] == jnp.arange(capacity, dtype=jnp.int32)[None, None, :]
+    )
+    slot_hit = jnp.transpose(place_hit, (1, 2, 0)).reshape(slot_count, group_size)
+    dispatch = slot_hit.astype(jnp.bfloat16)
+    combine = jnp.where(
+        slot_hit, jnp.repeat(weight_of.T, capacity, axis=0), 0.0
+    )
     outgoing = jnp.dot(dispatch, group_rows, preferred_element_type=jnp.float32).astype(
         jnp.bfloat16
     )
     outgoing = outgoing.reshape(expert_count, local_experts, capacity, model_width)
-    combine = jnp.sum(jnp.where(hit, group_weights[None, :, :], 0.0), axis=2)
     combine_hi = combine.astype(jnp.bfloat16)
     combine_lo = (combine - combine_hi.astype(jnp.float32)).astype(jnp.bfloat16)
     stacked = jnp.concatenate([combine_hi, combine_lo], axis=1)

time: 255 us -> 252 us (0.988)
  no operation moved by 1% of the time
where the time goes in v9:
time: 252 us; the launch traced here: 251 us
  blocking collectives  228 us (90%)
  Pallas kernels  12.4 us (5%)
  matrix products  4.91 us (2%)
  other arithmetic  3.13 us (1%)
    all_to_all x1, blocking collectives, body(): lax.all_to_all(outgoing, 'expert', split_axis=0, concat_axis=0, tiled=True)  102 us
    all_to_all x1, blocking collectives, body(): lax.all_to_all(partial_rows, 'expert', split_axis=0, concat_axis=0, tiled...  101 us
    all_to_all x1, blocking collectives, body(): lax.all_to_all(pieces, 'dp', split_axis=0, concat_axis=0, tiled=True)  25.8 us
    pallas_call x1, Pallas kernels, expert_ffn(): pl.pallas_call(ffn_block, grid=(local_experts, sources // per_step), in_s...  12.4 us

profile of v9, /device:TPU:11, one launch (start us, length us, event | category | flops | bytes accessed | tf_op | source)
XLA Modules:
  0.0 250.6 jit_solution(10807660081932233520)
XLA Ops:
  0.0 0.8 copy.14
  0.8 0.2 fusion.14
  0.9 0.2 convolution_convert_fusion.1
  1.1 0.1 copy.15
  1.2 0.8 copy.16
  2.0 0.2 select_reduce_fusion
  2.2 0.1 copy.17
  2.3 0.1 eq.54
  2.4 0.1 fusion.12
  2.5 0.2 fusion.9
  2.7 0.2 fusion.8
  2.9 1.2 fusion
  4.2 0.2 pad_maximum_fusion
  4.4 3.4 %convolution_convert_fusion = bf16[1024,4096]{1,0:T(8,128)(2,1)S(1)} fusion(pred[1024,64]{1,0:T(8,128)(4,1)S(1)} %bitcast.46, bf16[1,64,4096]{2,1,0:T(8,128)(2,1)} %param.7, f32[4096]{0:T(1024)} %param.8, f32[64]{0:T(128)S(1)} %add_rsqrt_fusion), kind=kOutput, calls=%fused_computation | convolution fusion | flops 542113792 | bytes 8995072 | tf_op jit(solution)/shard_map/dot_general | solution.py:70
  7.8 101.7 %all_to_all.15.x_ref = bf16[32,2,16,4096]{3,2,1,0:T(8,128)(2,1)} all-to-all(bf16[32,2,16,4096]{3,2,1,0:T(8,128)(2,1)S(1)} %bitcast.44), channel_id=1, replica_groups=mesh['dp'=8,'expert'=32] {'expert'}, dimensions={0} | all-to-all | bytes 16777216 | tf_op jit(solution)/shard_map/all_to_all | solution.py:78
  109.5 12.4 %shard_map.73 = bf16[32,2,16,4096]{3,2,1,0:T(8,128)(2,1)} custom-call(bf16[32,2,16,4096]{3,2,1,0:T(8,128)(2,1)} %all_to_all.15.x_ref, bf16[2,192,4096]{2,1,0:T(8,128)(2,1)} %gate_ref.1, bf16[2,192,4096]{2,1,0:T(8,128)(2,1)} %up_ref.1, bf16[2,192,4096]{2,1,0:T(8,128)(2,1)} %down_ref.1), custom_call_target="tpu_custom_call" | custom-call | flops 4831838208 | bytes 26214400 | tf_op jit(solution)/shard_map/pallas_call | solution.py:26
  122.0 100.7 %all_to_all.16 = bf16[32,2,16,4096]{3,2,1,0:T(8,128)(2,1)S(1)} all-to-all(bf16[32,2,16,4096]{3,2,1,0:T(8,128)(2,1)} %shard_map.73), channel_id=1, replica_groups=mesh['dp'=8,'expert'=32] {'expert'}, dimensions={0} | all-to-all | bytes 16777216 | tf_op jit(solution)/shard_map/all_to_all | solution.py:80
  222.7 1.3 fusion.16
  224.0 0.1 fusion.4
  224.1 25.8 %all_to_all.17 = bf16[8,8,4096]{2,1,0:T(8,128)(2,1)S(1)} all-to-all(bf16[8,8,4096]{2,1,0:T(8,128)(2,1)S(1)} %fusion.4), channel_id=1, replica_groups=mesh['dp'=8,'expert'=32] {'dp'}, dimensions={0} | all-to-all | bytes 1048576 | tf_op jit(solution)/shard_map/all_to_all | solution.py:86
  249.9 0.7 reduce_sum.32
  (2 shorter events, 0.0 us)

commit v10 on v9

--- a/solution.py
+++ b/solution.py
@@ -53,9 +53,13 @@
     tok_float = tokens[0].astype(jnp.float32)
     inv_rms = lax.rsqrt(jnp.mean(tok_float * tok_float, axis=-1, keepdims=True) + 1e-06)
     group_rows = (tok_float * inv_rms * norm_gain).astype(jnp.bfloat16)
-    chosen = group_ids[:, :, None] == jnp.arange(experts, dtype=jnp.int32)[None, None, :]
-    picks = jnp.any(chosen, axis=1)
-    weight_of = jnp.sum(jnp.where(chosen, group_weights[:, :, None], 0.0), axis=1)
+    expert_at = jnp.arange(experts, dtype=jnp.int32)[None, :]
+    picks = jnp.zeros((group_size, experts), jnp.bool_)
+    weight_of = jnp.zeros((group_size, experts), jnp.float32)
+    for choice in range(top_k):
+        named = group_ids[:, choice : choice + 1] == expert_at
+        picks = picks | named
+        weight_of = weight_of + jnp.where(named, group_weights[:, choice : choice + 1], 0.0)
     token_at = jnp.arange(group_size, dtype=jnp.int32)
     earlier = (token_at[:, None] > token_at[None, :]).astype(jnp.bfloat16)
     rank = jnp.dot(earlier, picks.astype(jnp.bfloat16), preferred_element_type=jnp.float32)

time: 252 us -> 252 us (level)
  no operation moved by 1% of the time
where the time goes in v10:
time: 252 us; the launch traced here: 251 us
  blocking collectives  228 us (90%)
  Pallas kernels  12.4 us (5%)
  matrix products  5.04 us (2%)
  other arithmetic  2.81 us (1%)
    all_to_all x1, blocking collectives, body(): lax.all_to_all(outgoing, 'expert', split_axis=0, concat_axis=0, tiled=True)  102 us
    all_to_all x1, blocking collectives, body(): lax.all_to_all(partial_rows, 'expert', split_axis=0, concat_axis=0, tiled...  101 us
    all_to_all x1, blocking collectives, body(): lax.all_to_all(pieces, 'dp', split_axis=0, concat_axis=0, tiled=True)  25.8 us
    pallas_call x1, Pallas kernels, expert_ffn(): pl.pallas_call(ffn_block, grid=(local_experts, sources // per_step), in_s...  12.4 us

profile of v10, /device:TPU:11, one launch (start us, length us, event | category | flops | bytes accessed | tf_op | source)
XLA Modules:
  0.0 250.6 jit_solution(9746394463847858539)
XLA Ops:
  0.0 1.0 slice_bitcast_fusion.15
  1.0 0.3 convolution_convert_fusion.1
  1.3 1.0 slice_bitcast_fusion.7
  2.3 0.1 eq.286
  2.4 0.1 fusion.12
  2.6 0.2 fusion.9
  2.8 0.2 fusion.8
  3.0 1.2 fusion
  4.3 0.2 pad_maximum_fusion
  4.4 3.4 %convolution_convert_fusion = bf16[1024,4096]{1,0:T(8,128)(2,1)S(1)} fusion(pred[1024,64]{1,0:T(8,128)(4,1)S(1)} %bitcast.76, bf16[1,64,4096]{2,1,0:T(8,128)(2,1)} %param.7, f32[4096]{0:T(1024)} %param.8, f32[64]{0:T(128)S(1)} %add_rsqrt_fusion), kind=kOutput, calls=%fused_computation | convolution fusion | flops 542113792 | bytes 8995072 | tf_op jit(solution)/shard_map/dot_general | solution.py:74
  7.9 101.7 %all_to_all.15.x_ref = bf16[32,2,16,4096]{3,2,1,0:T(8,128)(2,1)} all-to-all(bf16[32,2,16,4096]{3,2,1,0:T(8,128)(2,1)S(1)} %bitcast.74), channel_id=1, replica_groups=mesh['dp'=8,'expert'=32] {'expert'}, dimensions={0} | all-to-all | bytes 16777216 | tf_op jit(solution)/shard_map/all_to_all | solution.py:82
  109.6 12.4 %shard_map.73 = bf16[32,2,16,4096]{3,2,1,0:T(8,128)(2,1)} custom-call(bf16[32,2,16,4096]{3,2,1,0:T(8,128)(2,1)} %all_to_all.15.x_ref, bf16[2,192,4096]{2,1,0:T(8,128)(2,1)} %gate_ref.1, bf16[2,192,4096]{2,1,0:T(8,128)(2,1)} %up_ref.1, bf16[2,192,4096]{2,1,0:T(8,128)(2,1)} %down_ref.1), custom_call_target="tpu_custom_call" | custom-call | flops 4831838208 | bytes 26214400 | tf_op jit(solution)/shard_map/pallas_call | solution.py:26
  122.0 100.7 %all_to_all.16 = bf16[32,2,16,4096]{3,2,1,0:T(8,128)(2,1)S(1)} all-to-all(bf16[32,2,16,4096]{3,2,1,0:T(8,128)(2,1)} %shard_map.73), channel_id=1, replica_groups=mesh['dp'=8,'expert'=32] {'expert'}, dimensions={0} | all-to-all | bytes 16777216 | tf_op jit(solution)/shard_map/all_to_all | solution.py:84
  222.8 1.3 fusion.38
  224.0 0.1 fusion.4
  224.2 25.8 %all_to_all.17 = bf16[8,8,4096]{2,1,0:T(8,128)(2,1)S(1)} all-to-all(bf16[8,8,4096]{2,1,0:T(8,128)(2,1)S(1)} %fusion.4), channel_id=1, replica_groups=mesh['dp'=8,'expert'=32] {'dp'}, dimensions={0} | all-to-all | bytes 1048576 | tf_op jit(solution)/shard_map/all_to_all | solution.py:90
  249.9 0.7 reduce_sum.22
  (4 shorter events, 0.1 us)

commit v11 on v10

--- a/solution.py
+++ b/solution.py
@@ -2,33 +2,40 @@
 import jax.numpy as jnp
 from jax import lax
 from jax.experimental import pallas as pl
+from jax.experimental.pallas import tpu as pltpu
 from jax.sharding import PartitionSpec as P
 
 
-def ffn_block(x_ref, gate_ref, up_ref, down_ref, out_ref):
-    width = x_ref.shape[3]
-    rows = x_ref[...].reshape(x_ref.shape[0] * x_ref.shape[2], width)
-    contract = (((1,), (1,)), ((), ()))
-    gate_act = lax.dot_general(rows, gate_ref[0], contract, preferred_element_type=jnp.float32)
-    up_act = lax.dot_general(rows, up_ref[0], contract, preferred_element_type=jnp.float32)
-    hidden = (gate_act / (1.0 + jnp.exp(-gate_act)) * up_act).astype(jnp.bfloat16)
-    partial = jnp.dot(hidden, down_ref[0], preferred_element_type=jnp.float32)
+def ffn_block(x_ref, gate_ref, up_ref, down_ref, out_ref, hidden_ref):
+    @pl.when(pl.program_id(1) == 0)
+    def _():
+        width = x_ref.shape[3]
+        rows = x_ref[...].reshape(x_ref.shape[0] * x_ref.shape[2], width)
+        contract = (((1,), (1,)), ((), ()))
+        gate_act = lax.dot_general(rows, gate_ref[0], contract, preferred_element_type=jnp.float32)
+        up_act = lax.dot_general(rows, up_ref[0], contract, preferred_element_type=jnp.float32)
+        hidden_ref[...] = (gate_act / (1.0 + jnp.exp(-gate_act)) * up_act).astype(jnp.bfloat16)
+
+    partial = jnp.dot(hidden_ref[...], down_ref[0], preferred_element_type=jnp.float32)
     out_ref[...] = partial.astype(out_ref.dtype).reshape(out_ref.shape)
 
 
 def expert_ffn(incoming, gate_proj, up_proj, down_proj):
     sources, local_experts, capacity, width = incoming.shape
     hidden_width = gate_proj.shape[1]
-    per_step = 32
-    row_spec = pl.BlockSpec((per_step, 1, capacity, width), lambda j, b: (b, j, 0, 0))
-    weight_spec = pl.BlockSpec((1, hidden_width, width), lambda j, b: (j, 0, 0))
+    halves = 2
     rows = sources * local_experts * capacity
+    x_spec = pl.BlockSpec((sources, 1, capacity, width), lambda j, c: (0, j, 0, 0))
+    weight_spec = pl.BlockSpec((1, hidden_width, width), lambda j, c: (j, 0, 0))
+    down_spec = pl.BlockSpec((1, hidden_width, width // halves), lambda j, c: (j, 0, c))
+    out_spec = pl.BlockSpec((sources, 1, capacity, width // halves), lambda j, c: (0, j, 0, c))
     return pl.pallas_call(
         ffn_block,
-        grid=(local_experts, sources // per_step),
-        in_specs=[row_spec, weight_spec, weight_spec, weight_spec],
-        out_specs=row_spec,
+        grid=(local_experts, halves),
+        in_specs=[x_spec, weight_spec, weight_spec, down_spec],
+        out_specs=out_spec,
         out_shape=jax.ShapeDtypeStruct(incoming.shape, jnp.bfloat16),
+        scratch_shapes=[pltpu.VMEM((sources * capacity, hidden_width), jnp.bfloat16)],
         cost_estimate=pl.CostEstimate(
             flops=6 * rows * hidden_width * width,
             transcendentals=rows * hidden_width,
@@ -51,7 +58,11 @@
     capacity = dp_count * (group_size * top_k // (experts * dp_count) + 1)
     slot_count = experts * capacity
     tok_float = tokens[0].astype(jnp.float32)
-    inv_rms = lax.rsqrt(jnp.mean(tok_float * tok_float, axis=-1, keepdims=True) + 1e-06)
+    gram = lax.dot_general(
+        tokens[0], tokens[0], (((1,), (1,)), ((), ())), preferred_element_type=jnp.float32
+    )
+    squares = jnp.sum(jnp.where(jnp.eye(gram.shape[0], dtype=jnp.bool_), gram, 0.0), axis=1)
+    inv_rms = lax.rsqrt(squares[:, None] / model_width + 1e-06)
     group_rows = (tok_float * inv_rms * norm_gain).astype(jnp.bfloat16)
     expert_at = jnp.arange(experts, dtype=jnp.int32)[None, :]
     picks = jnp.zeros((group_size, experts), jnp.bool_)

time: 252 us -> 257 us (1.020)
  Pallas kernels: 12.4 us -> 16.3 us
    pallas_call x1, Pallas kernels: 12.4 us -> 16.3 us  [expert_ffn(): pl.pallas_call(ffn_block, grid=(local_experts, halves), in_specs=[x_spec,...]
where the time goes in v11:
time: 257 us; the launch traced here: 255 us
  blocking collectives  228 us (89%)
  Pallas kernels  16.3 us (6%)
  matrix products  6.54 us (3%)
    all_to_all x1, blocking collectives, body(): lax.all_to_all(outgoing, 'expert', split_axis=0, concat_axis=0, tiled=True)  102 us
    all_to_all x1, blocking collectives, body(): lax.all_to_all(partial_rows, 'expert', split_axis=0, concat_axis=0, tiled...  101 us
    all_to_all x1, blocking collectives, body(): lax.all_to_all(pieces, 'dp', split_axis=0, concat_axis=0, tiled=True)  25.8 us
    pallas_call x1, Pallas kernels, expert_ffn(): pl.pallas_call(ffn_block, grid=(local_experts, halves), in_specs=[x_spec,...  16.3 us

profile of v11, /device:TPU:11, one launch (start us, length us, event | category | flops | bytes accessed | tf_op | source)
XLA Modules:
  0.0 255.2 jit_solution(6999919446244621035)
XLA Ops:
  0.0 1.0 slice_bitcast_fusion.15
  1.0 0.1 fusion.13
  1.1 0.3 convolution_convert_fusion.1
  1.4 1.0 slice_bitcast_fusion.7
  2.4 0.1 copy.10
  2.5 0.2 select_add_fusion
  2.7 0.1 copy.11
  2.8 0.1 eq.289
  2.9 0.1 fusion.11
  3.0 0.2 fusion.8
  3.2 0.2 fusion.7
  3.5 1.5 fusion
  5.0 0.1 pad_maximum_fusion
  5.1 3.4 %convolution_convert_fusion = bf16[1024,4096]{1,0:T(8,128)(2,1)S(1)} fusion(pred[1024,64]{1,0:T(8,128)(4,1)S(1)} %bitcast.79, bf16[1,64,4096]{2,1,0:T(8,128)(2,1)} %param.7, f32[4096]{0:T(1024)} %param.8, f32[64]{0:T(128)S(1)} %add_rsqrt_fusion), kind=kOutput, calls=%fused_computation | convolution fusion | flops 542113792 | bytes 8995072 | tf_op jit(solution)/shard_map/dot_general | solution.py:85
  8.6 101.7 %all_to_all.15.x_ref = bf16[32,2,16,4096]{3,2,1,0:T(8,128)(2,1)} all-to-all(bf16[32,2,16,4096]{3,2,1,0:T(8,128)(2,1)S(1)} %bitcast.77), channel_id=1, replica_groups=mesh['dp'=8,'expert'=32] {'expert'}, dimensions={0} | all-to-all | bytes 16777216 | tf_op jit(solution)/shard_map/all_to_all | solution.py:93
  110.3 16.3 %shard_map.73 = bf16[32,2,16,4096]{3,2,1,0:T(8,128)(2,1)} custom-call(bf16[32,2,16,4096]{3,2,1,0:T(8,128)(2,1)} %all_to_all.15.x_ref, bf16[2,192,4096]{2,1,0:T(8,128)(2,1)} %gate_ref.1, bf16[2,192,4096]{2,1,0:T(8,128)(2,1)} %up_ref.1, bf16[2,192,4096]{2,1,0:T(8,128)(2,1)} %down_ref.1), custom_call_target="tpu_custom_call" | custom-call | flops 4831838208 | bytes 26214400 | tf_op jit(solution)/shard_map/pallas_call | solution.py:32
  126.6 100.7 %all_to_all.16 = bf16[32,2,16,4096]{3,2,1,0:T(8,128)(2,1)S(1)} all-to-all(bf16[32,2,16,4096]{3,2,1,0:T(8,128)(2,1)} %shard_map.73), channel_id=1, replica_groups=mesh['dp'=8,'expert'=32] {'expert'}, dimensions={0} | all-to-all | bytes 16777216 | tf_op jit(solution)/shard_map/all_to_all | solution.py:95
  227.4 1.3 fusion.37
  228.7 0.1 fusion.4
  228.8 25.8 %all_to_all.17 = bf16[8,8,4096]{2,1,0:T(8,128)(2,1)S(1)} all-to-all(bf16[8,8,4096]{2,1,0:T(8,128)(2,1)S(1)} %fusion.4), channel_id=1, replica_groups=mesh['dp'=8,'expert'=32] {'dp'}, dimensions={0} | all-to-all | bytes 1048576 | tf_op jit(solution)/shard_map/all_to_all | solution.py:101
  254.5 0.7 reduce_sum.22
  (2 shorter events, 0.0 us)

commit v12 on v10

--- a/solution.py
+++ b/solution.py
@@ -2,17 +2,21 @@
 import jax.numpy as jnp
 from jax import lax
 from jax.experimental import pallas as pl
+from jax.experimental.pallas import tpu as pltpu
 from jax.sharding import PartitionSpec as P
 
 
-def ffn_block(x_ref, gate_ref, up_ref, down_ref, out_ref):
+def ffn_block(x_ref, gate_ref, up_ref, down_hbm, out_ref, down_buf, down_sem):
+    fetch = pltpu.make_async_copy(down_hbm.at[pl.program_id(0)], down_buf, down_sem)
+    fetch.start()
     width = x_ref.shape[3]
     rows = x_ref[...].reshape(x_ref.shape[0] * x_ref.shape[2], width)
     contract = (((1,), (1,)), ((), ()))
     gate_act = lax.dot_general(rows, gate_ref[0], contract, preferred_element_type=jnp.float32)
     up_act = lax.dot_general(rows, up_ref[0], contract, preferred_element_type=jnp.float32)
     hidden = (gate_act / (1.0 + jnp.exp(-gate_act)) * up_act).astype(jnp.bfloat16)
-    partial = jnp.dot(hidden, down_ref[0], preferred_element_type=jnp.float32)
+    fetch.wait()
+    partial = jnp.dot(hidden, down_buf[...], preferred_element_type=jnp.float32)
     out_ref[...] = partial.astype(out_ref.dtype).reshape(out_ref.shape)
 
 
@@ -26,9 +30,13 @@
     return pl.pallas_call(
         ffn_block,
         grid=(local_experts, sources // per_step),
-        in_specs=[row_spec, weight_spec, weight_spec, weight_spec],
+        in_specs=[row_spec, weight_spec, weight_spec, pl.BlockSpec(memory_space=pl.ANY)],
         out_specs=row_spec,
         out_shape=jax.ShapeDtypeStruct(incoming.shape, jnp.bfloat16),
+        scratch_shapes=[
+            pltpu.VMEM((hidden_width, width), down_proj.dtype),
+            pltpu.SemaphoreType.DMA(()),
+        ],
         cost_estimate=pl.CostEstimate(
             flops=6 * rows * hidden_width * width,
             transcendentals=rows * hidden_width,

time: 252 us -> 253 us (level)
  no operation moved by 1% of the time
where the time goes in v12:
time: 253 us; the launch traced here: 251 us
  blocking collectives  228 us (90%)
  Pallas kernels  13 us (5%)
  matrix products  5.03 us (2%)
  other arithmetic  2.81 us (1%)
    all_to_all x1, blocking collectives, body(): lax.all_to_all(outgoing, 'expert', split_axis=0, concat_axis=0, tiled=True)  102 us
    all_to_all x1, blocking collectives, body(): lax.all_to_all(partial_rows, 'expert', split_axis=0, concat_axis=0, tiled...  101 us
    all_to_all x1, blocking collectives, body(): lax.all_to_all(pieces, 'dp', split_axis=0, concat_axis=0, tiled=True)  25.8 us
    pallas_call x1, Pallas kernels, expert_ffn(): pl.pallas_call(ffn_block, grid=(local_experts, sources // per_step), in_s...  13 us

profile of v12, /device:TPU:11, one launch (start us, length us, event | category | flops | bytes accessed | tf_op | source)
XLA Modules:
  0.0 251.2 jit_solution(7046024892147469564)
XLA Ops:
  0.0 1.0 slice_bitcast_fusion.15
  1.0 0.3 convolution_convert_fusion.1
  1.3 1.0 slice_bitcast_fusion.7
  2.3 0.1 eq.286
  2.4 0.1 fusion.12
  2.6 0.2 fusion.9
  2.8 0.2 fusion.8
  3.0 1.2 fusion
  4.3 0.2 pad_maximum_fusion
  4.4 3.4 %convolution_convert_fusion = bf16[1024,4096]{1,0:T(8,128)(2,1)S(1)} fusion(pred[1024,64]{1,0:T(8,128)(4,1)S(1)} %bitcast.76, bf16[1,64,4096]{2,1,0:T(8,128)(2,1)} %param.7, f32[4096]{0:T(1024)} %param.8, f32[64]{0:T(128)S(1)} %add_rsqrt_fusion), kind=kOutput, calls=%fused_computation | convolution fusion | flops 542113792 | bytes 8995072 | tf_op jit(solution)/shard_map/dot_general | solution.py:82
  7.9 101.7 %all_to_all.15.x_ref = bf16[32,2,16,4096]{3,2,1,0:T(8,128)(2,1)} all-to-all(bf16[32,2,16,4096]{3,2,1,0:T(8,128)(2,1)S(1)} %bitcast.74), channel_id=1, replica_groups=mesh['dp'=8,'expert'=32] {'expert'}, dimensions={0} | all-to-all | bytes 16777216 | tf_op jit(solution)/shard_map/all_to_all | solution.py:90
  109.6 13.0 %shard_map.73 = bf16[32,2,16,4096]{3,2,1,0:T(8,128)(2,1)} custom-call(bf16[32,2,16,4096]{3,2,1,0:T(8,128)(2,1)} %all_to_all.15.x_ref, bf16[2,192,4096]{2,1,0:T(8,128)(2,1)} %gate_ref.1, bf16[2,192,4096]{2,1,0:T(8,128)(2,1)} %up_ref.1, bf16[2,192,4096]{2,1,0:T(8,128)(2,1)} %down_hbm.1), custom_call_target="tpu_custom_call" | custom-call | flops 4831838208 | bytes 26214400 | tf_op jit(solution)/shard_map/pallas_call | solution.py:30
  122.5 100.8 %all_to_all.16 = bf16[32,2,16,4096]{3,2,1,0:T(8,128)(2,1)S(1)} all-to-all(bf16[32,2,16,4096]{3,2,1,0:T(8,128)(2,1)} %shard_map.73), channel_id=1, replica_groups=mesh['dp'=8,'expert'=32] {'expert'}, dimensions={0} | all-to-all | bytes 16777216 | tf_op jit(solution)/shard_map/all_to_all | solution.py:92
  223.3 1.3 fusion.38
  224.6 0.1 fusion.4
  224.7 25.8 %all_to_all.17 = bf16[8,8,4096]{2,1,0:T(8,128)(2,1)S(1)} all-to-all(bf16[8,8,4096]{2,1,0:T(8,128)(2,1)S(1)} %fusion.4), channel_id=1, replica_groups=mesh['dp'=8,'expert'=32] {'dp'}, dimensions={0} | all-to-all | bytes 1048576 | tf_op jit(solution)/shard_map/all_to_all | solution.py:98
  250.4 0.7 reduce_sum.22
  (4 shorter events, 0.1 us)
